TPU v7x, 32 devices: a whole 2x2x4 slice. The times are simulated.
32 devices in a mesh: group: 2 (over y), ctx: 4 (over z), head: 2 (over x), sub: 2 (over core).
Axes of the slice: x: 2, y: 2, z: 4, core: 2. Of those that a mesh axis runs over, the one named last changes fastest.
Arguments:
- queries: bfloat16 [4, 4096, 128], P(('head', 'sub'), ('group', 'ctx')), parts along dimension 1, may hold values from -18 to 18
- keys: bfloat16 [4, 4096, 128], P(('head', 'sub'), ('group', 'ctx')), parts along dimension 1, may hold values from -6 to 6
- values: bfloat16 [4, 4096, 128], P(('head', 'sub'), ('group', 'ctx')), parts along dimension 1, may hold values from -6 to 6
- stick_offset: float32 [4], P(('head', 'sub')), may hold values from -14 to -7
Outputs:
- attended: bfloat16 [4, 4096, 128], P(('head', 'sub'), ('group', 'ctx')), parts along dimension 1
There are 2 independent parts, one for each index of `group`. A program takes and returns all parts, laid end to end along the dimension named above; an argument that names none is the same for every part. Nothing has to cross between parts.
All inputs are finite; a program needn't handle non-finite values.
Results may differ from a plain program's by a relative error of at most 0.0049.
Values may be sent and summed in bfloat16 or wider, within the bound.
No kernel may reach another device: no remote copies, remote signals or barrier semaphores. Data moves between devices by JAX's collectives and lax.ppermute only.
A program may use at most 64 MiB of HBM per device.

v0:
```python
import functools
import math

import jax
import numpy as np
import jax.numpy as jnp
from jax import lax
from jax.experimental import pallas as pl
from jax.experimental.pallas import tpu as pltpu
from jax.sharding import PartitionSpec as P


ROW_TILE = 256
LOG2E = 1.4426950408889634
LN2 = 0.6931471805599453


def pair_kernel(scalar_ref, q_ref, kv_ref, upper_ref, *refs, mode, scale):
    diag = mode == "diag"
    if mode in ("step", "final"):
        in_summed_ref, in_spent_ref, summed_ref, spent_ref = refs
    else:
        summed_ref = refs[0]
    tile, _ = q_ref.shape
    keys = kv_ref.shape[0] // 2
    score = (
        lax.dot_general(
            q_ref[...],
            kv_ref[:keys, :],
            (((1,), (1,)), ((), ())),
            preferred_element_type=jnp.float32,
        )
        * (scale * LOG2E)
        + scalar_ref[0] * LOG2E
    )
    spent = jnp.maximum(score, 0.0) + jnp.log2(1.0 + jnp.exp2(-jnp.abs(score)))
    if diag:
        row = pl.program_id(0) * tile + lax.broadcasted_iota(jnp.int32, (tile, keys), 0)
        col = lax.broadcasted_iota(jnp.int32, (tile, keys), 1)
        live = col < row
        spent = jnp.where(live, spent, 0.0)
    upper = upper_ref[...]
    high = spent.astype(jnp.bfloat16)
    low = (spent - high.astype(jnp.float32)).astype(jnp.bfloat16)
    later = jnp.dot(high, upper, preferred_element_type=jnp.float32) + jnp.dot(
        low, upper, preferred_element_type=jnp.float32
    )
    weight = jnp.exp2((score - spent) - later)
    if diag:
        weight = jnp.where(live, weight, 0.0)
    part = jnp.dot(weight.astype(jnp.bfloat16), kv_ref[keys:, :], preferred_element_type=jnp.float32)
    if mode == "far":
        summed_ref[...] = part.astype(summed_ref.dtype)
        return
    tot = (later[:, 0:1] + spent[:, 0:1]) * LN2
    if diag:
        summed_ref[...] = part
        refs[1][...] = tot
        return
    use = scalar_ref[1] > 0.0
    before = in_spent_ref[...]
    summed_ref[...] = jnp.where(use, in_summed_ref[...] + jnp.exp(-before) * part, in_summed_ref[...])
    after = jnp.where(use, before + tot, before)
    if mode == "final":
        spent_ref[...] = jnp.broadcast_to(jnp.exp(-after), spent_ref.shape)
    else:
        spent_ref[...] = after


def payload_kernel(flag_ref, q_ref, k_ref, v_ref, own_ref, sent_ref):
    rows = k_ref.shape[0]
    own_ref[:rows, :] = k_ref[...]
    own_ref[rows:, :] = v_ref[...]
    sent_ref[rows:, :] = v_ref[...]

    @pl.when(flag_ref[0] > 0.0)
    def _():
        sent_ref[:rows, :] = q_ref[...]

    @pl.when(flag_ref[0] <= 0.0)
    def _():
        sent_ref[:rows, :] = k_ref[...]


def payloads(flag, q, k, v):
    rows, width = k.shape
    block = pl.BlockSpec((rows, width), lambda i: (0, 0))
    both = pl.BlockSpec((2 * rows, width), lambda i: (0, 0))
    shape = jax.ShapeDtypeStruct((2 * rows, width), k.dtype)
    return pl.pallas_call(
        payload_kernel,
        grid=(1,),
        in_specs=[pl.BlockSpec(memory_space=pltpu.SMEM), block, block, block],
        out_specs=[both, both],
        out_shape=[shape, shape],
    )(flag, q, k, v)


def pair_terms(q, kv, upper, scalars, carried=None, mode="step", rows=None):
    width = q.shape[1]
    rows = q.shape[0] if rows is None else rows
    keys = kv.shape[0] // 2
    tile = min(ROW_TILE, rows)
    kernel = functools.partial(pair_kernel, mode=mode, scale=1.0 / math.sqrt(width))
    flops = 2 * rows * keys * (2 * width + 2 * keys)
    rows_spec = pl.BlockSpec((tile, width), lambda r: (r, 0))
    col_spec = pl.BlockSpec((tile, 1), lambda r: (r, 0))
    in_specs = [
        pl.BlockSpec(memory_space=pltpu.SMEM),
        rows_spec,
        pl.BlockSpec(memory_space=pltpu.VMEM),
        pl.BlockSpec(memory_space=pltpu.VMEM),
    ]
    args = [scalars, q, kv, upper]
    if mode in ("step", "final"):
        in_specs += [rows_spec, col_spec]
        args += list(carried)
    out_specs = [rows_spec]
    out_shape = [jax.ShapeDtypeStruct((rows, width), jnp.bfloat16 if mode == "far" else jnp.float32)]
    if mode == "final":
        out_specs.append(rows_spec)
        out_shape.append(jax.ShapeDtypeStruct((rows, width), jnp.float32))
    elif mode != "far":
        out_specs.append(col_spec)
        out_shape.append(jax.ShapeDtypeStruct((rows, 1), jnp.float32))
    return pl.pallas_call(
        kernel,
        grid=(rows // tile,),
        in_specs=in_specs,
        out_specs=out_specs,
        out_shape=out_shape,
        cost_estimate=pl.CostEstimate(
            flops=flops, transcendentals=3 * rows * keys, bytes_accessed=rows * width * 16
        ),
    )(*args)


def one_head(q_own, k_own, v_own, offset):
    count = lax.axis_size("ctx")
    place = lax.axis_index("ctx")
    up = [(i, (i + 1) % count) for i in range(count)]
    down = [(i, (i - 1) % count) for i in range(count)]
    rows = q_own.shape[0]
    keys = k_own.shape[0]
    upper = jnp.asarray(np.triu(np.ones((keys, keys), np.float32), 1).T, jnp.bfloat16)
    steps = jnp.arange(count, dtype=jnp.int32)
    table = jnp.stack(
        [jnp.broadcast_to(offset, (count,)), jnp.where(place >= steps, 1.0, 0.0)], axis=1
    ).astype(jnp.float32)
    last = place == count - 1
    own_kv, sent = payloads(jnp.where(last, 1.0, 0.0).reshape(1), q_own, k_own, v_own)
    summed, spent = pair_terms(q_own, own_kv, upper, table[0], mode="diag")
    if count == 1:
        return summed.astype(jnp.bfloat16)
    if count == 2:
        kv = lax.ppermute(own_kv, "ctx", up)
        summed, spent = pair_terms(q_own, kv, upper, table[1], (summed, spent))
        return summed.astype(jnp.bfloat16)
    kv = lax.ppermute(sent, "ctx", up)
    far = pair_terms(kv, own_kv, upper, table[0], mode="far", rows=rows)[0]
    for step in range(1, count - 1):
        if step > 1:
            kv = lax.ppermute(kv, "ctx", up)
        if step < count - 2:
            summed, spent = pair_terms(q_own, kv, upper, table[step], (summed, spent))
    far = lax.ppermute(far, "ctx", down)
    summed, scale = pair_terms(q_own, kv, upper, table[count - 2], (summed, spent), mode="final")
    out = jnp.where(last, summed + scale * far.astype(jnp.float32), summed)
    return out.astype(jnp.bfloat16)


def on_device(queries, keys, values, stick_offset):
    results = []
    for h in range(queries.shape[0]):
        results.append(one_head(queries[h], keys[h], values[h], stick_offset[h]))
    return jnp.stack(results, axis=0)


def solution(mesh):
    placed = (
        P(("head", "sub"), ("group", "ctx"), None),
        P(("head", "sub"), ("group", "ctx"), None),
        P(("head", "sub"), ("group", "ctx"), None),
        P(("head", "sub")),
    )
    return jax.shard_map(
        on_device,
        mesh=mesh,
        in_specs=placed,
        out_specs=P(("head", "sub"), ("group", "ctx"), None),
        check_vma=False,
    )
```

profile of v0, /device:TPU:0, one launch (start us, length us, event | category | flops | bytes accessed | tf_op | source)
XLA Modules:
  0.0 35.0 jit_solution(1761231753226788088)
XLA Ops:
  0.0 1.9 %shard_map.55 = (bf16[1024,128]{1,0:T(8,128)(2,1)}, bf16[1024,128]{1,0:T(8,128)(2,1)}) custom-call(f32[1]{0:T(128)} %bitcast.3.flag_ref, bf16[512,128]{1,0:T(8,128)(2,1)} %bitcast.16, bf16[512,128]{1,0:T(8,128)(2,1)} %bitcast.14, bf16[512,128]{1,0:T(8,128)(2,1)} %bitcast.15), custom_call_target="tpu_custom_call" | custom-call | tf_op jit(solution)/shard_map/pallas_call | solution.py:90
  1.9 3.1 %collective-permute-start = (bf16[1024,128]{1,0:T(8,128)(2,1)}, bf16[1024,128]{1,0:T(8,128)(2,1)S(1)}, u32[]{:S(2)}, u32[]{:S(2)}) collective-permute-start(bf16[1024,128]{1,0:T(8,128)(2,1)} %get-tuple-element.13), channel_id=1, source_target_pairs={{0,4},{4,8},{8,12},{12,0},{1,5},{5,9},{9,13},{13,1},{2,6},{6,10},{... | collective-permute-start | bytes 786440 | tf_op jit(solution)/shard_map/ppermute | solution.py:159
  5.6 7.9 %collective-permute-done.kv_ref.q_ref = bf16[1024,128]{1,0:T(8,128)(2,1)S(1)} collective-permute-done((bf16[1024,128]{1,0:T(8,128)(2,1)}, bf16[1024,128]{1,0:T(8,128)(2,1)S(1)}, u32[]{:S(2)}, u32[]{:S(2)}) %collective-permute-start) | collective-permute-done | bytes 262176 | tf_op jit(solution)/shard_map/ppermute | solution.py:159
  13.5 0.0 copy-start
  13.5 0.0 collective-permute-start.1
  13.5 0.7 %fusion.5 = (f32[2]{0:T(128)}, f32[2]{0:T(128)}, f32[2]{0:T(128)}) fusion(f32[4,1]{1,0:T(4,128)S(1)} %fusion.2, f32[]{:T(128)} %bitcast.13), kind=kLoop, calls=%fused_computation.10 | loop fusion | bytes 44 | tf_op jit(solution)/shard_map/squeeze | solution.py:152
  14.1 0.0 copy-done
  14.2 3.5 %shard_map.59 = bf16[512,128]{1,0:T(8,128)(2,1)} custom-call(f32[2]{0:T(128)} %get-tuple-element.21.scalar_ref, bf16[1024,128]{1,0:T(8,128)(2,1)} %copy-done, bf16[1024,128]{1,0:T(8,128)(2,1)} %get-tuple-element.14.kv_ref, bf16[512,512]{1,0:T(8,128)(2,1)} %constant.13.clone.upper_ref), custom_call_target="tpu_custom_call" | custom-call | flops 671088640 | bytes 1048576 | tf_op jit(solution)/shard_map/pallas_call | solution.py:126
  17.6 3.8 %collective-permute-start.2 = (bf16[512,128]{1,0:T(8,128)(2,1)}, bf16[512,128]{1,0:T(8,128)(2,1)S(1)}, u32[]{:S(2)}, u32[]{:S(2)}) collective-permute-start(bf16[512,128]{1,0:T(8,128)(2,1)} %shard_map.59), channel_id=1, source_target_pairs={{0,12},{4,0},{8,4},{12,8},{1,13},{5,1},{9,5},{13,9},{2,14},{6,2},{... | collective-permute-start | bytes 393224 | tf_op jit(solution)/shard_map/ppermute | solution.py:166
  21.4 3.6 %shard_map.56 = (f32[512,128]{1,0:T(8,128)}, f32[512,1]{1,0:T(8,128)}) custom-call(f32[2]{0:T(128)} %get-tuple-element.21.scalar_ref, bf16[512,128]{1,0:T(8,128)(2,1)} %bitcast.17, bf16[1024,128]{1,0:T(8,128)(2,1)} %get-tuple-element.14.kv_ref, bf16[512,512]{1,0:T(8,128)(2,1)} %constant.13.clone.upper_ref), custom_call_target="tpu_custom_call" | custom-call | flops 671088640 | bytes 1048576 | tf_op jit(solution)/shard_map/pallas_call | solution.py:126
  25.0 3.8 %shard_map.57 = (f32[512,128]{1,0:T(8,128)}, f32[512,1]{1,0:T(8,128)}) custom-call(f32[2]{0:T(128)} %get-tuple-element.22.scalar_ref, bf16[512,128]{1,0:T(8,128)(2,1)} %bitcast.18, bf16[1024,128]{1,0:T(8,128)(2,1)} %copy-done, bf16[512,512]{1,0:T(8,128)(2,1)} %constant.13.clone.upper_ref, f32[512,128]{1,0:T(8,128)} %get-tuple-element.15.refs_0_, ...), custom_call_target="tpu_custom_call" | custom-call | flops 671088640 | bytes 1048576 | tf_op jit(solution)/shard_map/pallas_call | solution.py:126
  28.8 0.0 collective-permute-done.1.kv_ref
  28.8 0.0 copy-start.1
  28.8 0.7 %copy-done.1 = bf16[1024,128]{1,0:T(8,128)(2,1)} copy-done((bf16[1024,128]{1,0:T(8,128)(2,1)}, bf16[1024,128]{1,0:T(8,128)(2,1)S(1)}, u32[]{:S(2)}) %copy-start.1) | copy-done | bytes 262168
  29.5 3.7 %shard_map.58 = (f32[512,128]{1,0:T(8,128)}, f32[512,128]{1,0:T(8,128)}) custom-call(f32[2]{0:T(128)} %get-tuple-element.23.scalar_ref, bf16[512,128]{1,0:T(8,128)(2,1)} %bitcast.19, bf16[1024,128]{1,0:T(8,128)(2,1)} %copy-done.1, bf16[512,512]{1,0:T(8,128)(2,1)} %constant.13.clone.upper_ref, f32[512,128]{1,0:T(8,128)} %get-tuple-element.17.refs_0_, ...), custom_call_target="tpu_custom_call" | custom-call | flops 671088640 | bytes 1048576 | tf_op jit(solution)/shard_map/pallas_call | solution.py:126
  33.2 0.0 collective-permute-done.2
  33.2 1.7 %fusion.1 = bf16[1,512,128]{2,1,0:T(8,128)(2,1)} fusion(f32[512,128]{1,0:T(8,128)} %get-tuple-element.19, f32[512,128]{1,0:T(8,128)} %get-tuple-element.20, bf16[512,128]{1,0:T(8,128)(2,1)S(1)} %collective-permute-done.2, pred[]{:T(512)S(6)} %eq.3), kind=kLoop, calls=%fused_computation.2 | loop fusion | flops 327680 | bytes 786433 | tf_op jit(solution)/shard_map/stack | solution.py:176
  (1 shorter events, 0.0 us)
Async XLA Ops:
  1.9 11.6 %collective-permute-start = (bf16[1024,128]{1,0:T(8,128)(2,1)}, bf16[1024,128]{1,0:T(8,128)(2,1)S(1)}, u32[]{:S(2)}, u32[]{:S(2)}) collective-permute-start(bf16[1024,128]{1,0:T(8,128)(2,1)} %get-tuple-element.13), channel_id=1, source_target_pairs={{0,4},{4,8},{8,12},{12,0},{1,5},{5,9},{9,13},{13,1},{2,6},{6,10},{... | collective-permute-start | bytes 786440 | tf_op jit(solution)/shard_map/ppermute | solution.py:159
  13.5 0.7 %copy-start = (bf16[1024,128]{1,0:T(8,128)(2,1)}, bf16[1024,128]{1,0:T(8,128)(2,1)S(1)}, u32[]{:S(2)}) copy-start(bf16[1024,128]{1,0:T(8,128)(2,1)S(1)} %collective-permute-done.kv_ref.q_ref) | copy-start | bytes 786436
  13.5 15.3 %collective-permute-start.1 = (bf16[1024,128]{1,0:T(8,128)(2,1)S(1)}, bf16[1024,128]{1,0:T(8,128)(2,1)S(1)}, u32[]{:S(2)}, u32[]{:S(2)}) collective-permute-start(bf16[1024,128]{1,0:T(8,128)(2,1)S(1)} %collective-permute-done.kv_ref.q_ref), channel_id=1, source_target_pairs={{0,4},{4,8},{8,12},{12,0},{1,5},{5,9},{9,13},{13,1},{2,6},{6,10},{... | collective-permute-start | bytes 786440 | tf_op jit(solution)/shard_map/ppermute | solution.py:163
  17.6 15.6 %collective-permute-start.2 = (bf16[512,128]{1,0:T(8,128)(2,1)}, bf16[512,128]{1,0:T(8,128)(2,1)S(1)}, u32[]{:S(2)}, u32[]{:S(2)}) collective-permute-start(bf16[512,128]{1,0:T(8,128)(2,1)} %shard_map.59), channel_id=1, source_target_pairs={{0,12},{4,0},{8,4},{12,8},{1,13},{5,1},{9,5},{13,9},{2,14},{6,2},{... | collective-permute-start | bytes 393224 | tf_op jit(solution)/shard_map/ppermute | solution.py:166
  28.8 0.7 %copy-start.1 = (bf16[1024,128]{1,0:T(8,128)(2,1)}, bf16[1024,128]{1,0:T(8,128)(2,1)S(1)}, u32[]{:S(2)}) copy-start(bf16[1024,128]{1,0:T(8,128)(2,1)S(1)} %collective-permute-done.1.kv_ref) | copy-start | bytes 786436
where the time goes:
time: 35.2 us; the launch traced here: 35 us
  Pallas kernels  16.4 us (47%)
  waiting for transfers between devices  7.88 us (22%)
  starting transfers between devices  6.84 us (19%)
  other arithmetic  1.74 us (5%)
  local copies, waits for them, and re-layouts  1.39 us (4%)
  between operations  0.68 us (2%)
    pallas_call x4, Pallas kernels, pair_terms(): pl.pallas_call(kernel, grid=(rows // tile,), in_specs=in_specs, out_specs...  14.6 us
    ppermute x1, waiting for transfers between devices, one_head(): kv = lax.ppermute(sent, 'ctx', up)  7.87 us
    ppermute x1, starting transfers between devices, one_head(): far = lax.ppermute(far, 'ctx', down)  3.78 us
    ppermute x1, starting transfers between devices, one_head(): kv = lax.ppermute(sent, 'ctx', up)  3.05 us
    pallas_call x1, Pallas kernels, payloads(): pl.pallas_call(payload_kernel, grid=(1,), in_specs=[pl.BlockSpec(memory_s...  1.88 us
    another operation x1, other arithmetic, on_device(): return jnp.stack(results, axis=0)  1.73 us
    unnamed x4, local copies, waits for them, and re-layouts  0.73 us
  transfers between devices with their start and end apart: 3, of which 1 were waited for; matrix products, arithmetic and copies ran while one was open for 2% of the time, Pallas kernels for 42%

commit v1 on v0

--- a/solution.py
+++ b/solution.py
@@ -15,13 +15,19 @@
 LN2 = 0.6931471805599453
 
 
-def pair_kernel(scalar_ref, q_ref, kv_ref, upper_ref, *refs, mode, scale):
+def pair_kernel(scalar_ref, q_ref, kv_ref, upper_ref, *refs, mode, scale, rows, tile):
+    for r in range(rows // tile):
+        pair_rows(scalar_ref, q_ref, kv_ref, upper_ref, refs, mode, scale, r, tile)
+
+
+def pair_rows(scalar_ref, q_all, kv_ref, upper_ref, refs, mode, scale, r, tile):
     diag = mode == "diag"
+    rs = slice(r * tile, (r + 1) * tile)
     if mode in ("step", "final"):
-        in_summed_ref, in_spent_ref, summed_ref, spent_ref = refs
+        in_summed_ref, in_spent_ref, summed_ref, spent_ref = (ref.at[rs] for ref in refs)
     else:
-        summed_ref = refs[0]
-    tile, _ = q_ref.shape
+        summed_ref = refs[0].at[rs]
+    q_ref = q_all.at[rs]
     keys = kv_ref.shape[0] // 2
     score = (
         lax.dot_general(
@@ -35,7 +41,7 @@
     )
     spent = jnp.maximum(score, 0.0) + jnp.log2(1.0 + jnp.exp2(-jnp.abs(score)))
     if diag:
-        row = pl.program_id(0) * tile + lax.broadcasted_iota(jnp.int32, (tile, keys), 0)
+        row = r * tile + lax.broadcasted_iota(jnp.int32, (tile, keys), 0)
         col = lax.broadcasted_iota(jnp.int32, (tile, keys), 1)
         live = col < row
         spent = jnp.where(live, spent, 0.0)
@@ -55,7 +61,7 @@
     tot = (later[:, 0:1] + spent[:, 0:1]) * LN2
     if diag:
         summed_ref[...] = part
-        refs[1][...] = tot
+        refs[1].at[rs][...] = tot
         return
     use = scalar_ref[1] > 0.0
     before = in_spent_ref[...]
@@ -101,31 +107,26 @@
     rows = q.shape[0] if rows is None else rows
     keys = kv.shape[0] // 2
     tile = min(ROW_TILE, rows)
-    kernel = functools.partial(pair_kernel, mode=mode, scale=1.0 / math.sqrt(width))
+    kernel = functools.partial(
+        pair_kernel, mode=mode, scale=1.0 / math.sqrt(width), rows=rows, tile=tile
+    )
     flops = 2 * rows * keys * (2 * width + 2 * keys)
-    rows_spec = pl.BlockSpec((tile, width), lambda r: (r, 0))
-    col_spec = pl.BlockSpec((tile, 1), lambda r: (r, 0))
-    in_specs = [
-        pl.BlockSpec(memory_space=pltpu.SMEM),
-        rows_spec,
-        pl.BlockSpec(memory_space=pltpu.VMEM),
-        pl.BlockSpec(memory_space=pltpu.VMEM),
-    ]
+    vmem = pl.BlockSpec(memory_space=pltpu.VMEM)
+    in_specs = [pl.BlockSpec(memory_space=pltpu.SMEM), vmem, vmem, vmem]
     args = [scalars, q, kv, upper]
     if mode in ("step", "final"):
-        in_specs += [rows_spec, col_spec]
+        in_specs += [vmem, vmem]
         args += list(carried)
-    out_specs = [rows_spec]
+    out_specs = [vmem]
     out_shape = [jax.ShapeDtypeStruct((rows, width), jnp.bfloat16 if mode == "far" else jnp.float32)]
     if mode == "final":
-        out_specs.append(rows_spec)
+        out_specs.append(vmem)
         out_shape.append(jax.ShapeDtypeStruct((rows, width), jnp.float32))
     elif mode != "far":
-        out_specs.append(col_spec)
+        out_specs.append(vmem)
         out_shape.append(jax.ShapeDtypeStruct((rows, 1), jnp.float32))
     return pl.pallas_call(
         kernel,
-        grid=(rows // tile,),
         in_specs=in_specs,
         out_specs=out_specs,
         out_shape=out_shape,

time: 35.2 us -> 34.4 us (0.977)
  Pallas kernels: 16.4 us -> 15.6 us
    pallas_call x4, Pallas kernels: 14.6 us -> 13.7 us  [pair_terms(): pl.pallas_call(kernel, in_specs=in_specs, out_specs=out_specs, out_shape=...]
  transfers between devices with their start and end apart: 3 -> 3, of which waited for: 1 -> 1; matrix products, arithmetic and copies ran while one was open for 2% -> 2% of each run, Pallas kernels for 42% -> 40%
where the time goes in v1:
time: 34.4 us; the launch traced here: 34.1 us
  Pallas kernels  15.6 us (45%)
  waiting for transfers between devices  7.88 us (23%)
  starting transfers between devices  6.83 us (20%)
  other arithmetic  1.74 us (5%)
  local copies, waits for them, and re-layouts  1.39 us (4%)
  between operations  0.67 us (2%)
    pallas_call x4, Pallas kernels, pair_terms(): pl.pallas_call(kernel, in_specs=in_specs, out_specs=out_specs, out_shape=...  13.7 us
    ppermute x1, waiting for transfers between devices, one_head(): kv = lax.ppermute(sent, 'ctx', up)  7.87 us
    ppermute x1, starting transfers between devices, one_head(): far = lax.ppermute(far, 'ctx', down)  3.77 us
    ppermute x1, starting transfers between devices, one_head(): kv = lax.ppermute(sent, 'ctx', up)  3.05 us
    pallas_call x1, Pallas kernels, payloads(): pl.pallas_call(payload_kernel, grid=(1,), in_specs=[pl.BlockSpec(memory_s...  1.88 us
    another operation x1, other arithmetic, on_device(): return jnp.stack(results, axis=0)  1.73 us
    unnamed x4, local copies, waits for them, and re-layouts  0.74 us
  transfers between devices with their start and end apart: 3, of which 1 were waited for; matrix products, arithmetic and copies ran while one was open for 2% of the time, Pallas kernels for 40%

profile of v1, /device:TPU:0, one launch (start us, length us, event | category | flops | bytes accessed | tf_op | source)
XLA Modules:
  0.0 34.1 jit_solution(11510705340349219246)
XLA Ops:
  0.0 1.9 %shard_map.55 = (bf16[1024,128]{1,0:T(8,128)(2,1)}, bf16[1024,128]{1,0:T(8,128)(2,1)}) custom-call(f32[1]{0:T(128)} %bitcast.3.flag_ref, bf16[512,128]{1,0:T(8,128)(2,1)} %bitcast.16, bf16[512,128]{1,0:T(8,128)(2,1)} %bitcast.14, bf16[512,128]{1,0:T(8,128)(2,1)} %bitcast.15), custom_call_target="tpu_custom_call" | custom-call | tf_op jit(solution)/shard_map/pallas_call | solution.py:96
  1.9 3.1 %collective-permute-start = (bf16[1024,128]{1,0:T(8,128)(2,1)}, bf16[1024,128]{1,0:T(8,128)(2,1)S(1)}, u32[]{:S(2)}, u32[]{:S(2)}) collective-permute-start(bf16[1024,128]{1,0:T(8,128)(2,1)} %get-tuple-element.13), channel_id=1, source_target_pairs={{0,4},{4,8},{8,12},{12,0},{1,5},{5,9},{9,13},{13,1},{2,6},{6,10},{... | collective-permute-start | bytes 786440 | tf_op jit(solution)/shard_map/ppermute | solution.py:160
  5.6 7.9 %collective-permute-done.kv_ref.q_ref = bf16[1024,128]{1,0:T(8,128)(2,1)S(1)} collective-permute-done((bf16[1024,128]{1,0:T(8,128)(2,1)}, bf16[1024,128]{1,0:T(8,128)(2,1)S(1)}, u32[]{:S(2)}, u32[]{:S(2)}) %collective-permute-start) | collective-permute-done | bytes 262176 | tf_op jit(solution)/shard_map/ppermute | solution.py:160
  13.5 0.0 copy-start
  13.5 0.0 collective-permute-start.1
  13.5 0.7 %fusion.5 = (f32[2]{0:T(128)}, f32[2]{0:T(128)}, f32[2]{0:T(128)}) fusion(f32[4,1]{1,0:T(4,128)S(1)} %fusion.2, f32[]{:T(128)} %bitcast.13), kind=kLoop, calls=%fused_computation.10 | loop fusion | bytes 44 | tf_op jit(solution)/shard_map/squeeze | solution.py:153
  14.1 0.0 copy-done
  14.2 3.4 %shard_map.59 = bf16[512,128]{1,0:T(8,128)(2,1)} custom-call(f32[2]{0:T(128)} %get-tuple-element.21.scalar_ref, bf16[1024,128]{1,0:T(8,128)(2,1)} %copy-done, bf16[1024,128]{1,0:T(8,128)(2,1)} %get-tuple-element.14.kv_ref, bf16[512,512]{1,0:T(8,128)(2,1)} %constant.13.clone.upper_ref), custom_call_target="tpu_custom_call" | custom-call | flops 671088640 | bytes 1048576 | tf_op jit(solution)/shard_map/pallas_call | solution.py:128
  17.5 3.8 %collective-permute-start.2 = (bf16[512,128]{1,0:T(8,128)(2,1)}, bf16[512,128]{1,0:T(8,128)(2,1)S(1)}, u32[]{:S(2)}, u32[]{:S(2)}) collective-permute-start(bf16[512,128]{1,0:T(8,128)(2,1)} %shard_map.59), channel_id=1, source_target_pairs={{0,12},{4,0},{8,4},{12,8},{1,13},{5,1},{9,5},{13,9},{2,14},{6,2},{... | collective-permute-start | bytes 393224 | tf_op jit(solution)/shard_map/ppermute | solution.py:167
  21.3 3.3 %shard_map.56 = (f32[512,128]{1,0:T(8,128)}, f32[512,1]{1,0:T(8,128)}) custom-call(f32[2]{0:T(128)} %get-tuple-element.21.scalar_ref, bf16[512,128]{1,0:T(8,128)(2,1)} %bitcast.17, bf16[1024,128]{1,0:T(8,128)(2,1)} %get-tuple-element.14.kv_ref, bf16[512,512]{1,0:T(8,128)(2,1)} %constant.13.clone.upper_ref), custom_call_target="tpu_custom_call" | custom-call | flops 671088640 | bytes 1048576 | tf_op jit(solution)/shard_map/pallas_call | solution.py:128
  24.6 3.5 %shard_map.57 = (f32[512,128]{1,0:T(8,128)}, f32[512,1]{1,0:T(8,128)}) custom-call(f32[2]{0:T(128)} %get-tuple-element.22.scalar_ref, bf16[512,128]{1,0:T(8,128)(2,1)} %bitcast.18, bf16[1024,128]{1,0:T(8,128)(2,1)} %copy-done, bf16[512,512]{1,0:T(8,128)(2,1)} %constant.13.clone.upper_ref, f32[512,128]{1,0:T(8,128)} %get-tuple-element.15.refs_0_, ...), custom_call_target="tpu_custom_call" | custom-call | flops 671088640 | bytes 1048576 | tf_op jit(solution)/shard_map/pallas_call | solution.py:128
  28.1 0.0 collective-permute-done.1.kv_ref
  28.1 0.0 copy-start.1
  28.1 0.7 %copy-done.1 = bf16[1024,128]{1,0:T(8,128)(2,1)} copy-done((bf16[1024,128]{1,0:T(8,128)(2,1)}, bf16[1024,128]{1,0:T(8,128)(2,1)S(1)}, u32[]{:S(2)}) %copy-start.1) | copy-done | bytes 262168
  28.8 3.6 %shard_map.58 = (f32[512,128]{1,0:T(8,128)}, f32[512,128]{1,0:T(8,128)}) custom-call(f32[2]{0:T(128)} %get-tuple-element.23.scalar_ref, bf16[512,128]{1,0:T(8,128)(2,1)} %bitcast.19, bf16[1024,128]{1,0:T(8,128)(2,1)} %copy-done.1, bf16[512,512]{1,0:T(8,128)(2,1)} %constant.13.clone.upper_ref, f32[512,128]{1,0:T(8,128)} %get-tuple-element.17.refs_0_, ...), custom_call_target="tpu_custom_call" | custom-call | flops 671088640 | bytes 1048576 | tf_op jit(solution)/shard_map/pallas_call | solution.py:128
  32.4 0.0 collective-permute-done.2
  32.4 1.7 %fusion.1 = bf16[1,512,128]{2,1,0:T(8,128)(2,1)} fusion(f32[512,128]{1,0:T(8,128)} %get-tuple-element.19, f32[512,128]{1,0:T(8,128)} %get-tuple-element.20, bf16[512,128]{1,0:T(8,128)(2,1)S(1)} %collective-permute-done.2, pred[]{:T(512)S(6)} %eq.3), kind=kLoop, calls=%fused_computation.2 | loop fusion | flops 327680 | bytes 786433 | tf_op jit(solution)/shard_map/stack | solution.py:177
  (1 shorter events, 0.0 us)
Async XLA Ops:
  1.9 11.6 %collective-permute-start = (bf16[1024,128]{1,0:T(8,128)(2,1)}, bf16[1024,128]{1,0:T(8,128)(2,1)S(1)}, u32[]{:S(2)}, u32[]{:S(2)}) collective-permute-start(bf16[1024,128]{1,0:T(8,128)(2,1)} %get-tuple-element.13), channel_id=1, source_target_pairs={{0,4},{4,8},{8,12},{12,0},{1,5},{5,9},{9,13},{13,1},{2,6},{6,10},{... | collective-permute-start | bytes 786440 | tf_op jit(solution)/shard_map/ppermute | solution.py:160
  13.5 0.7 %copy-start = (bf16[1024,128]{1,0:T(8,128)(2,1)}, bf16[1024,128]{1,0:T(8,128)(2,1)S(1)}, u32[]{:S(2)}) copy-start(bf16[1024,128]{1,0:T(8,128)(2,1)S(1)} %collective-permute-done.kv_ref.q_ref) | copy-start | bytes 786436
  13.5 14.6 %collective-permute-start.1 = (bf16[1024,128]{1,0:T(8,128)(2,1)S(1)}, bf16[1024,128]{1,0:T(8,128)(2,1)S(1)}, u32[]{:S(2)}, u32[]{:S(2)}) collective-permute-start(bf16[1024,128]{1,0:T(8,128)(2,1)S(1)} %collective-permute-done.kv_ref.q_ref), channel_id=1, source_target_pairs={{0,4},{4,8},{8,12},{12,0},{1,5},{5,9},{9,13},{13,1},{2,6},{6,10},{... | collective-permute-start | bytes 786440 | tf_op jit(solution)/shard_map/ppermute | solution.py:164
  17.5 14.9 %collective-permute-start.2 = (bf16[512,128]{1,0:T(8,128)(2,1)}, bf16[512,128]{1,0:T(8,128)(2,1)S(1)}, u32[]{:S(2)}, u32[]{:S(2)}) collective-permute-start(bf16[512,128]{1,0:T(8,128)(2,1)} %shard_map.59), channel_id=1, source_target_pairs={{0,12},{4,0},{8,4},{12,8},{1,13},{5,1},{9,5},{13,9},{2,14},{6,2},{... | collective-permute-start | bytes 393224 | tf_op jit(solution)/shard_map/ppermute | solution.py:167
  28.1 0.7 %copy-start.1 = (bf16[1024,128]{1,0:T(8,128)(2,1)}, bf16[1024,128]{1,0:T(8,128)(2,1)S(1)}, u32[]{:S(2)}) copy-start(bf16[1024,128]{1,0:T(8,128)(2,1)S(1)} %collective-permute-done.1.kv_ref) | copy-start | bytes 786436

commit v2 on v1

--- a/solution.py
+++ b/solution.py
@@ -15,12 +15,12 @@
 LN2 = 0.6931471805599453
 
 
-def pair_kernel(scalar_ref, q_ref, kv_ref, upper_ref, *refs, mode, scale, rows, tile):
+def pair_kernel(scalar_ref, q_ref, k_ref, v_ref, upper_ref, *refs, mode, scale, rows, tile, offsets):
     for r in range(rows // tile):
-        pair_rows(scalar_ref, q_ref, kv_ref, upper_ref, refs, mode, scale, r, tile)
-
-
-def pair_rows(scalar_ref, q_all, kv_ref, upper_ref, refs, mode, scale, r, tile):
+        pair_rows(scalar_ref, q_ref, k_ref, v_ref, upper_ref, refs, mode, scale, r, tile, offsets)
+
+
+def pair_rows(scalar_ref, q_all, k_ref, v_ref, upper_ref, refs, mode, scale, r, tile, offsets):
     diag = mode == "diag"
     rs = slice(r * tile, (r + 1) * tile)
     if mode in ("step", "final"):
@@ -28,11 +28,12 @@
     else:
         summed_ref = refs[0].at[rs]
     q_ref = q_all.at[rs]
-    keys = kv_ref.shape[0] // 2
+    keys = upper_ref.shape[0]
+    k_at, v_at = offsets
     score = (
         lax.dot_general(
             q_ref[...],
-            kv_ref[:keys, :],
+            k_ref[k_at : k_at + keys, :],
             (((1,), (1,)), ((), ())),
             preferred_element_type=jnp.float32,
         )
@@ -54,7 +55,9 @@
     weight = jnp.exp2((score - spent) - later)
     if diag:
         weight = jnp.where(live, weight, 0.0)
-    part = jnp.dot(weight.astype(jnp.bfloat16), kv_ref[keys:, :], preferred_element_type=jnp.float32)
+    part = jnp.dot(
+        weight.astype(jnp.bfloat16), v_ref[v_at : v_at + keys, :], preferred_element_type=jnp.float32
+    )
     if mode == "far":
         summed_ref[...] = part.astype(summed_ref.dtype)
         return
@@ -73,10 +76,8 @@
         spent_ref[...] = after
 
 
-def payload_kernel(flag_ref, q_ref, k_ref, v_ref, own_ref, sent_ref):
+def payload_kernel(flag_ref, q_ref, k_ref, v_ref, sent_ref):
     rows = k_ref.shape[0]
-    own_ref[:rows, :] = k_ref[...]
-    own_ref[rows:, :] = v_ref[...]
     sent_ref[rows:, :] = v_ref[...]
 
     @pl.when(flag_ref[0] > 0.0)
@@ -92,28 +93,64 @@
     rows, width = k.shape
     block = pl.BlockSpec((rows, width), lambda i: (0, 0))
     both = pl.BlockSpec((2 * rows, width), lambda i: (0, 0))
-    shape = jax.ShapeDtypeStruct((2 * rows, width), k.dtype)
     return pl.pallas_call(
         payload_kernel,
         grid=(1,),
         in_specs=[pl.BlockSpec(memory_space=pltpu.SMEM), block, block, block],
-        out_specs=[both, both],
-        out_shape=[shape, shape],
+        out_specs=both,
+        out_shape=jax.ShapeDtypeStruct((2 * rows, width), k.dtype),
     )(flag, q, k, v)
+
+
+def finish_kernel(flag_ref, summed_ref, scale_ref, far_ref, out_ref):
+    summed = summed_ref[...]
+
+    @pl.when(flag_ref[0] > 0.0)
+    def _():
+        out_ref[...] = (summed + scale_ref[...] * far_ref[...].astype(jnp.float32)).astype(
+            out_ref.dtype
+        )
+
+    @pl.when(flag_ref[0] <= 0.0)
+    def _():
+        out_ref[...] = summed.astype(out_ref.dtype)
+
+
+def finished(flag, summed, scale, far):
+    rows, width = summed.shape
+    vmem = pl.BlockSpec(memory_space=pltpu.VMEM)
+    return pl.pallas_call(
+        finish_kernel,
+        grid=(1,),
+        in_specs=[pl.BlockSpec(memory_space=pltpu.SMEM), vmem, vmem, vmem],
+        out_specs=pl.BlockSpec((rows, width), lambda i: (0, 0)),
+        out_shape=jax.ShapeDtypeStruct((rows, width), jnp.bfloat16),
+    )(flag, summed, scale, far)
 
 
 def pair_terms(q, kv, upper, scalars, carried=None, mode="step", rows=None):
     width = q.shape[1]
     rows = q.shape[0] if rows is None else rows
-    keys = kv.shape[0] // 2
+    keys = upper.shape[0]
     tile = min(ROW_TILE, rows)
+    if isinstance(kv, tuple):
+        k, v = kv
+        offsets = (0, 0)
+    else:
+        k = v = kv
+        offsets = (0, keys)
     kernel = functools.partial(
-        pair_kernel, mode=mode, scale=1.0 / math.sqrt(width), rows=rows, tile=tile
+        pair_kernel,
+        mode=mode,
+        scale=1.0 / math.sqrt(width),
+        rows=rows,
+        tile=tile,
+        offsets=offsets,
     )
     flops = 2 * rows * keys * (2 * width + 2 * keys)
     vmem = pl.BlockSpec(memory_space=pltpu.VMEM)
-    in_specs = [pl.BlockSpec(memory_space=pltpu.SMEM), vmem, vmem, vmem]
-    args = [scalars, q, kv, upper]
+    in_specs = [pl.BlockSpec(memory_space=pltpu.SMEM), vmem, vmem, vmem, vmem]
+    args = [scalars, q, k, v, upper]
     if mode in ("step", "final"):
         in_specs += [vmem, vmem]
         args += list(carried)
@@ -149,7 +186,9 @@
         [jnp.broadcast_to(offset, (count,)), jnp.where(place >= steps, 1.0, 0.0)], axis=1
     ).astype(jnp.float32)
     last = place == count - 1
-    own_kv, sent = payloads(jnp.where(last, 1.0, 0.0).reshape(1), q_own, k_own, v_own)
+    flag = jnp.where(last, 1.0, 0.0).reshape(1).astype(jnp.float32)
+    own_kv = (k_own, v_own)
+    sent = payloads(flag, q_own, k_own, v_own)
     summed, spent = pair_terms(q_own, own_kv, upper, table[0], mode="diag")
     if count == 1:
         return summed.astype(jnp.bfloat16)
@@ -166,8 +205,7 @@
             summed, spent = pair_terms(q_own, kv, upper, table[step], (summed, spent))
     far = lax.ppermute(far, "ctx", down)
     summed, scale = pair_terms(q_own, kv, upper, table[count - 2], (summed, spent), mode="final")
-    out = jnp.where(last, summed + scale * far.astype(jnp.float32), summed)
-    return out.astype(jnp.bfloat16)
+    return finished(flag, summed, scale, far)
 
 
 def on_device(queries, keys, values, stick_offset):

time: 34.4 us -> 35.2 us (1.023)
  Pallas kernels: 15.6 us -> 17.5 us
  other arithmetic: 1.74 us -> 0.01 us
  local copies, waits for them, and re-layouts: 1.39 us -> 2.05 us
    pallas_call x0 -> x1, Pallas kernels: none -> 1.74 us  [finished(): pl.pallas_call(finish_kernel, grid=(1,), in_specs=[pl.BlockSpec(memory_sp...]
    another operation x1 -> x0, other arithmetic: 1.73 us -> none  [on_device(): return jnp.stack(results, axis=0)]
    unnamed x4 -> x6, local copies, waits for them, and re-layouts: 0.74 us -> 1.37 us
where the time goes in v2:
time: 35.2 us; the launch traced here: 34.9 us
  Pallas kernels  17.5 us (50%)
  waiting for transfers between devices  7.88 us (22%)
  starting transfers between devices  6.84 us (19%)
  local copies, waits for them, and re-layouts  2.05 us (6%)
  between operations  0.68 us (2%)
    pallas_call x4, Pallas kernels, pair_terms(): pl.pallas_call(kernel, in_specs=in_specs, out_specs=out_specs, out_shape=...  14 us
    ppermute x1, waiting for transfers between devices, one_head(): kv = lax.ppermute(sent, 'ctx', up)  7.88 us
    ppermute x1, starting transfers between devices, one_head(): far = lax.ppermute(far, 'ctx', down)  3.78 us
    ppermute x1, starting transfers between devices, one_head(): kv = lax.ppermute(sent, 'ctx', up)  3.05 us
    pallas_call x1, Pallas kernels, payloads(): pl.pallas_call(payload_kernel, grid=(1,), in_specs=[pl.BlockSpec(memory_s...  1.75 us
    pallas_call x1, Pallas kernels, finished(): pl.pallas_call(finish_kernel, grid=(1,), in_specs=[pl.BlockSpec(memory_sp...  1.74 us
    unnamed x6, local copies, waits for them, and re-layouts  1.37 us
  transfers between devices with their start and end apart: 3, of which 1 were waited for; matrix products, arithmetic and copies ran while one was open for 2% of the time, Pallas kernels for 40%

profile of v2, /device:TPU:0, one launch (start us, length us, event | category | flops | bytes accessed | tf_op | source)
XLA Modules:
  0.0 34.9 jit_solution(2014322104784943925)
XLA Ops:
  0.0 1.7 %shard_map.55 = bf16[1024,128]{1,0:T(8,128)(2,1)} custom-call(f32[1]{0:T(128)} %bitcast.flag_ref, bf16[512,128]{1,0:T(8,128)(2,1)} %bitcast.19, bf16[512,128]{1,0:T(8,128)(2,1)} %bitcast.13, bf16[512,128]{1,0:T(8,128)(2,1)} %bitcast.16), custom_call_target="tpu_custom_call" | custom-call | tf_op jit(solution)/shard_map/pallas_call | solution.py:96
  1.7 3.1 %collective-permute-start = (bf16[1024,128]{1,0:T(8,128)(2,1)}, bf16[1024,128]{1,0:T(8,128)(2,1)S(1)}, u32[]{:S(2)}, u32[]{:S(2)}) collective-permute-start(bf16[1024,128]{1,0:T(8,128)(2,1)} %shard_map.55), channel_id=1, source_target_pairs={{0,4},{4,8},{8,12},{12,0},{1,5},{5,9},{9,13},{13,1},{2,6},{6,10},{... | collective-permute-start | bytes 786440 | tf_op jit(solution)/shard_map/ppermute | solution.py:199
  5.5 7.9 %collective-permute-done.k_ref.v_ref.q_ref = bf16[1024,128]{1,0:T(8,128)(2,1)S(1)} collective-permute-done((bf16[1024,128]{1,0:T(8,128)(2,1)}, bf16[1024,128]{1,0:T(8,128)(2,1)S(1)}, u32[]{:S(2)}, u32[]{:S(2)}) %collective-permute-start) | collective-permute-done | bytes 262176 | tf_op jit(solution)/shard_map/ppermute | solution.py:199
  13.3 0.0 copy-start.1
  13.3 0.0 collective-permute-start.1
  13.3 0.7 %fusion.3 = (f32[2]{0:T(128)}, f32[2]{0:T(128)}, f32[2]{0:T(128)}) fusion(f32[4,1]{1,0:T(4,128)S(1)} %fusion, f32[]{:T(128)} %bitcast.12), kind=kLoop, calls=%fused_computation.7 | loop fusion | bytes 44 | tf_op jit(solution)/shard_map/squeeze | solution.py:192
  14.0 0.0 copy-done.1
  14.0 3.4 %shard_map.59 = bf16[512,128]{1,0:T(8,128)(2,1)} custom-call(f32[2]{0:T(128)} %get-tuple-element.17.scalar_ref, bf16[1024,128]{1,0:T(8,128)(2,1)} %copy-done.1, bf16[512,128]{1,0:T(8,128)(2,1)} %bitcast.14, bf16[512,128]{1,0:T(8,128)(2,1)} %bitcast.17, bf16[512,512]{1,0:T(8,128)(2,1)} %constant.13.clone.upper_ref), custom_call_target="tpu_custom_call" | custom-call | flops 671088640 | bytes 1048576 | tf_op jit(solution)/shard_map/pallas_call | solution.py:165
  17.5 3.8 %collective-permute-start.2 = (bf16[512,128]{1,0:T(8,128)(2,1)}, bf16[512,128]{1,0:T(8,128)(2,1)S(1)}, u32[]{:S(2)}, u32[]{:S(2)}) collective-permute-start(bf16[512,128]{1,0:T(8,128)(2,1)} %shard_map.59), channel_id=1, source_target_pairs={{0,12},{4,0},{8,4},{12,8},{1,13},{5,1},{9,5},{13,9},{2,14},{6,2},{... | collective-permute-start | bytes 393224 | tf_op jit(solution)/shard_map/ppermute | solution.py:206
  21.2 3.3 %shard_map.56 = (f32[512,128]{1,0:T(8,128)}, f32[512,1]{1,0:T(8,128)}) custom-call(f32[2]{0:T(128)} %get-tuple-element.17.scalar_ref, bf16[512,128]{1,0:T(8,128)(2,1)} %bitcast.20, bf16[512,128]{1,0:T(8,128)(2,1)} %bitcast.15, bf16[512,128]{1,0:T(8,128)(2,1)} %bitcast.18, bf16[512,512]{1,0:T(8,128)(2,1)} %constant.13.clone.upper_ref), custom_call_target="tpu_custom_call" | custom-call | flops 671088640 | bytes 1048576 | tf_op jit(solution)/shard_map/pallas_call | solution.py:165
  24.6 3.6 %shard_map.57 = (f32[512,128]{1,0:T(8,128)}, f32[512,1]{1,0:T(8,128)}) custom-call(f32[2]{0:T(128)} %get-tuple-element.18.scalar_ref, bf16[512,128]{1,0:T(8,128)(2,1)} %bitcast.21, bf16[1024,128]{1,0:T(8,128)(2,1)} %copy-done.1, bf16[1024,128]{1,0:T(8,128)(2,1)} %copy-done.1, bf16[512,512]{1,0:T(8,128)(2,1)} %constant.13.clone.upper_ref, ...), custom_call_target="tpu_custom_call" | custom-call | flops 671088640 | bytes 1048576 | tf_op jit(solution)/shard_map/pallas_call | solution.py:165
  28.2 0.0 collective-permute-done.1.k_ref.v_ref
  28.2 0.0 copy-start.2
  28.2 0.7 %copy-done.2 = bf16[1024,128]{1,0:T(8,128)(2,1)} copy-done((bf16[1024,128]{1,0:T(8,128)(2,1)}, bf16[1024,128]{1,0:T(8,128)(2,1)S(1)}, u32[]{:S(2)}) %copy-start.2) | copy-done | bytes 262168
  28.9 3.7 %shard_map.58 = (f32[512,128]{1,0:T(8,128)}, f32[512,128]{1,0:T(8,128)}) custom-call(f32[2]{0:T(128)} %get-tuple-element.19.scalar_ref, bf16[512,128]{1,0:T(8,128)(2,1)} %bitcast.22, bf16[1024,128]{1,0:T(8,128)(2,1)} %copy-done.2, bf16[1024,128]{1,0:T(8,128)(2,1)} %copy-done.2, bf16[512,512]{1,0:T(8,128)(2,1)} %constant.13.clone.upper_ref, ...), custom_call_target="tpu_custom_call" | custom-call | flops 671088640 | bytes 1048576 | tf_op jit(solution)/shard_map/pallas_call | solution.py:165
  32.5 0.0 collective-permute-done.2.far_ref
  32.5 0.0 copy-start
  32.6 0.6 %copy-done = bf16[512,128]{1,0:T(8,128)(2,1)} copy-done((bf16[512,128]{1,0:T(8,128)(2,1)}, bf16[512,128]{1,0:T(8,128)(2,1)S(1)}, u32[]{:S(2)}) %copy-start) | copy-done | bytes 131096
  33.2 1.7 %shard_map.60 = bf16[512,128]{1,0:T(8,128)(2,1)} custom-call(f32[1]{0:T(128)} %bitcast.flag_ref, f32[512,128]{1,0:T(8,128)} %get-tuple-element.15.summed_ref, f32[512,128]{1,0:T(8,128)} %get-tuple-element.16.scale_ref, bf16[512,128]{1,0:T(8,128)(2,1)} %copy-done), custom_call_target="tpu_custom_call" | custom-call | tf_op jit(solution)/shard_map/pallas_call | solution.py:122
  (1 shorter events, 0.0 us)
Async XLA Ops:
  1.7 11.6 %collective-permute-start = (bf16[1024,128]{1,0:T(8,128)(2,1)}, bf16[1024,128]{1,0:T(8,128)(2,1)S(1)}, u32[]{:S(2)}, u32[]{:S(2)}) collective-permute-start(bf16[1024,128]{1,0:T(8,128)(2,1)} %shard_map.55), channel_id=1, source_target_pairs={{0,4},{4,8},{8,12},{12,0},{1,5},{5,9},{9,13},{13,1},{2,6},{6,10},{... | collective-permute-start | bytes 786440 | tf_op jit(solution)/shard_map/ppermute | solution.py:199
  13.3 0.7 %copy-start.1 = (bf16[1024,128]{1,0:T(8,128)(2,1)}, bf16[1024,128]{1,0:T(8,128)(2,1)S(1)}, u32[]{:S(2)}) copy-start(bf16[1024,128]{1,0:T(8,128)(2,1)S(1)} %collective-permute-done.k_ref.v_ref.q_ref) | copy-start | bytes 786436
  13.3 14.8 %collective-permute-start.1 = (bf16[1024,128]{1,0:T(8,128)(2,1)S(1)}, bf16[1024,128]{1,0:T(8,128)(2,1)S(1)}, u32[]{:S(2)}, u32[]{:S(2)}) collective-permute-start(bf16[1024,128]{1,0:T(8,128)(2,1)S(1)} %collective-permute-done.k_ref.v_ref.q_ref), channel_id=1, source_target_pairs={{0,4},{4,8},{8,12},{12,0},{1,5},{5,9},{9,13},{13,1},{2,6},{6,10},{... | collective-permute-start | bytes 786440 | tf_op jit(solution)/shard_map/ppermute | solution.py:203
  17.5 15.1 %collective-permute-start.2 = (bf16[512,128]{1,0:T(8,128)(2,1)}, bf16[512,128]{1,0:T(8,128)(2,1)S(1)}, u32[]{:S(2)}, u32[]{:S(2)}) collective-permute-start(bf16[512,128]{1,0:T(8,128)(2,1)} %shard_map.59), channel_id=1, source_target_pairs={{0,12},{4,0},{8,4},{12,8},{1,13},{5,1},{9,5},{13,9},{2,14},{6,2},{... | collective-permute-start | bytes 393224 | tf_op jit(solution)/shard_map/ppermute | solution.py:206
  28.2 0.7 %copy-start.2 = (bf16[1024,128]{1,0:T(8,128)(2,1)}, bf16[1024,128]{1,0:T(8,128)(2,1)S(1)}, u32[]{:S(2)}) copy-start(bf16[1024,128]{1,0:T(8,128)(2,1)S(1)} %collective-permute-done.1.k_ref.v_ref) | copy-start | bytes 786436
  32.5 0.6 %copy-start = (bf16[512,128]{1,0:T(8,128)(2,1)}, bf16[512,128]{1,0:T(8,128)(2,1)S(1)}, u32[]{:S(2)}) copy-start(bf16[512,128]{1,0:T(8,128)(2,1)S(1)} %collective-permute-done.2.far_ref) | copy-start | bytes 393220

commit v3 on v1

--- a/solution.py
+++ b/solution.py
@@ -100,6 +100,65 @@
         out_specs=[both, both],
         out_shape=[shape, shape],
     )(flag, q, k, v)
+
+
+def fused_kernel(*refs, tasks, scale):
+    scalar_ref, upper_ref = refs[0], refs[1]
+    at = 2
+    ins = []
+    for mode, rows, tile in tasks:
+        take = 2 + (2 if mode in ("step", "final") else 0)
+        ins.append(refs[at : at + take])
+        at += take
+    for t, (mode, rows, tile) in enumerate(tasks):
+        q_ref, kv_ref = ins[t][:2]
+        carried = ins[t][2:]
+        take = 1 if mode == "far" else 2
+        outs = refs[at : at + take]
+        at += take
+        for r in range(rows // tile):
+            pair_rows(
+                scalar_ref.at[t], q_ref, kv_ref, upper_ref, tuple(carried) + tuple(outs),
+                mode, scale, r, tile,
+            )
+
+
+def fused_terms(upper, tasks):
+    vmem = pl.BlockSpec(memory_space=pltpu.VMEM)
+    keys = upper.shape[0]
+    scalars = jnp.stack([t["scalars"] for t in tasks])
+    args = [scalars, upper]
+    in_specs = [pl.BlockSpec(memory_space=pltpu.SMEM), vmem]
+    out_specs, out_shape, statics = [], [], []
+    flops = 0
+    for t in tasks:
+        q, kv, mode = t["q"], t["kv"], t["mode"]
+        width = q.shape[1]
+        rows = t.get("rows") or q.shape[0]
+        args += [q, kv]
+        in_specs += [vmem, vmem]
+        if mode in ("step", "final"):
+            args += list(t["carried"])
+            in_specs += [vmem, vmem]
+        out_specs.append(vmem)
+        out_shape.append(jax.ShapeDtypeStruct((rows, width), jnp.bfloat16 if mode == "far" else jnp.float32))
+        if mode != "far":
+            out_specs.append(vmem)
+            out_shape.append(
+                jax.ShapeDtypeStruct((rows, width) if mode == "final" else (rows, 1), jnp.float32)
+            )
+        statics.append((mode, rows, min(ROW_TILE, rows)))
+        flops += 2 * rows * keys * (2 * width + 2 * keys)
+    kernel = functools.partial(fused_kernel, tasks=tuple(statics), scale=1.0 / math.sqrt(width))
+    return pl.pallas_call(
+        kernel,
+        in_specs=in_specs,
+        out_specs=out_specs,
+        out_shape=out_shape,
+        cost_estimate=pl.CostEstimate(
+            flops=flops, transcendentals=3 * flops // (4 * width + 4 * keys), bytes_accessed=flops // 64
+        ),
+    )(*args)
 
 
 def pair_terms(q, kv, upper, scalars, carried=None, mode="step", rows=None):
@@ -158,14 +217,22 @@
         summed, spent = pair_terms(q_own, kv, upper, table[1], (summed, spent))
         return summed.astype(jnp.bfloat16)
     kv = lax.ppermute(sent, "ctx", up)
-    far = pair_terms(kv, own_kv, upper, table[0], mode="far", rows=rows)[0]
-    for step in range(1, count - 1):
-        if step > 1:
-            kv = lax.ppermute(kv, "ctx", up)
+    far_task = dict(q=kv, kv=own_kv, scalars=table[0], mode="far", rows=rows)
+    if count > 3:
+        far, summed, spent = fused_terms(
+            upper,
+            [far_task, dict(q=q_own, kv=kv, scalars=table[1], mode="step", carried=(summed, spent))],
+        )
+    else:
+        (far,) = fused_terms(upper, [far_task])
+    for step in range(2, count - 1):
+        kv = lax.ppermute(kv, "ctx", up)
         if step < count - 2:
             summed, spent = pair_terms(q_own, kv, upper, table[step], (summed, spent))
     far = lax.ppermute(far, "ctx", down)
-    summed, scale = pair_terms(q_own, kv, upper, table[count - 2], (summed, spent), mode="final")
+    summed, scale = pair_terms(
+        q_own, kv, upper, table[count - 2], (summed, spent), mode="final"
+    )
     out = jnp.where(last, summed + scale * far.astype(jnp.float32), summed)
     return out.astype(jnp.bfloat16)
 

time: 34.4 us -> 32.6 us (0.948)
  Pallas kernels: 15.6 us -> 13.9 us
  waiting for transfers between devices: 7.88 us -> 7.26 us
  local copies, waits for them, and re-layouts: 1.39 us -> 1.99 us
    pallas_call x4 -> x2, Pallas kernels: 13.7 us -> 6.89 us  [pair_terms(): pl.pallas_call(kernel, in_specs=in_specs, out_specs=out_specs, out_shape=...]
    pallas_call x0 -> x1, Pallas kernels: none -> 5.1 us  [fused_terms(): pl.pallas_call(kernel, in_specs=in_specs, out_specs=out_specs, out_shape=...]
    another operation x0 -> x1, local copies, waits for them, and re-layouts: none -> 0.68 us  [fused_terms(): scalars = jnp.stack([t['scalars'] for t in tasks])]
    ppermute x1, waiting for transfers between devices: 7.87 us -> 7.26 us  [one_head(): kv = lax.ppermute(sent, 'ctx', up)]
  transfers between devices with their start and end apart: 3 -> 3, of which waited for: 1 -> 1; matrix products, arithmetic and copies ran while one was open for 2% -> 4% of each run, Pallas kernels for 40% -> 37%
where the time goes in v3:
time: 32.6 us; the launch traced here: 32.4 us
  Pallas kernels  13.9 us (43%)
  waiting for transfers between devices  7.26 us (22%)
  starting transfers between devices  6.86 us (21%)
  local copies, waits for them, and re-layouts  1.99 us (6%)
  other arithmetic  1.74 us (5%)
  between operations  0.67 us (2%)
    ppermute x1, waiting for transfers between devices, one_head(): kv = lax.ppermute(sent, 'ctx', up)  7.26 us
    pallas_call x2, Pallas kernels, pair_terms(): pl.pallas_call(kernel, in_specs=in_specs, out_specs=out_specs, out_shape=...  6.89 us
    pallas_call x1, Pallas kernels, fused_terms(): pl.pallas_call(kernel, in_specs=in_specs, out_specs=out_specs, out_shape=...  5.1 us
    ppermute x1, starting transfers between devices, one_head(): far = lax.ppermute(far, 'ctx', down)  3.81 us
    ppermute x1, starting transfers between devices, one_head(): kv = lax.ppermute(sent, 'ctx', up)  3.05 us
    pallas_call x1, Pallas kernels, payloads(): pl.pallas_call(payload_kernel, grid=(1,), in_specs=[pl.BlockSpec(memory_s...  1.88 us
    another operation x1, other arithmetic, on_device(): return jnp.stack(results, axis=0)  1.73 us
    unnamed x4, local copies, waits for them, and re-layouts  0.7 us
  transfers between devices with their start and end apart: 3, of which 1 were waited for; matrix products, arithmetic and copies ran while one was open for 4% of the time, Pallas kernels for 37%

profile of v3, /device:TPU:0, one launch (start us, length us, event | category | flops | bytes accessed | tf_op | source)
XLA Modules:
  0.0 32.4 jit_solution(12575309614608817225)
XLA Ops:
  0.0 1.9 %shard_map.55 = (bf16[1024,128]{1,0:T(8,128)(2,1)}, bf16[1024,128]{1,0:T(8,128)(2,1)}) custom-call(f32[1]{0:T(128)} %bitcast.3.flag_ref, bf16[512,128]{1,0:T(8,128)(2,1)} %bitcast.15, bf16[512,128]{1,0:T(8,128)(2,1)} %bitcast.13, bf16[512,128]{1,0:T(8,128)(2,1)} %bitcast.14), custom_call_target="tpu_custom_call" | custom-call | tf_op jit(solution)/shard_map/pallas_call | solution.py:96
  1.9 3.1 %collective-permute-start = (bf16[1024,128]{1,0:T(8,128)(2,1)}, bf16[1024,128]{1,0:T(8,128)(2,1)S(1)}, u32[]{:S(2)}, u32[]{:S(2)}) collective-permute-start(bf16[1024,128]{1,0:T(8,128)(2,1)} %get-tuple-element.14), channel_id=1, source_target_pairs={{0,4},{4,8},{8,12},{12,0},{1,5},{5,9},{9,13},{13,1},{2,6},{6,10},{... | collective-permute-start | bytes 786440 | tf_op jit(solution)/shard_map/ppermute | solution.py:219
  5.6 0.6 %fusion.4 = (f32[2]{0:T(128)}, f32[2]{0:T(128)}) fusion(f32[4,1]{1,0:T(4,128)S(1)} %fusion.2, f32[]{:T(128)} %bitcast.12), kind=kLoop, calls=%fused_computation.9 | loop fusion | bytes 36 | tf_op jit(solution)/shard_map/squeeze | solution.py:212
  6.2 7.3 %collective-permute-done.refs_2_.refs_5_ = bf16[1024,128]{1,0:T(8,128)(2,1)S(1)} collective-permute-done((bf16[1024,128]{1,0:T(8,128)(2,1)}, bf16[1024,128]{1,0:T(8,128)(2,1)S(1)}, u32[]{:S(2)}, u32[]{:S(2)}) %collective-permute-start) | collective-permute-done | bytes 262176 | tf_op jit(solution)/shard_map/ppermute | solution.py:219
  13.5 0.0 copy-start
  13.5 0.0 collective-permute-start.1
  13.5 0.7 %pad_slice_fusion.1.refs_0_ = f32[2,2]{1,0:T(2,128)} fusion(f32[4,1]{1,0:T(4,128)S(1)} %fusion.2, f32[]{:T(128)} %bitcast.11), kind=kLoop, calls=%fused_computation.6 | loop fusion | bytes 36 | tf_op jit(solution)/shard_map/stack | solution.py:129
  14.2 3.3 %shard_map.56 = (f32[512,128]{1,0:T(8,128)}, f32[512,1]{1,0:T(8,128)}) custom-call(f32[2]{0:T(128)} %get-tuple-element.23.scalar_ref, bf16[512,128]{1,0:T(8,128)(2,1)} %bitcast.16, bf16[1024,128]{1,0:T(8,128)(2,1)} %get-tuple-element.15.kv_ref.refs_3_, bf16[512,512]{1,0:T(8,128)(2,1)} %constant.13.clone.upper_ref.refs_1_), custom_call_target="tpu_custom_call" | custom-call | flops 671088640 | bytes 1048576 | tf_op jit(solution)/shard_map/pallas_call | solution.py:187
  17.5 0.0 copy-done
  17.5 5.1 %shard_map.57 = (bf16[512,128]{1,0:T(8,128)(2,1)}, f32[512,128]{1,0:T(8,128)}, f32[512,1]{1,0:T(8,128)}) custom-call(f32[2,2]{1,0:T(2,128)} %pad_slice_fusion.1.refs_0_, bf16[512,512]{1,0:T(8,128)(2,1)} %constant.13.clone.upper_ref.refs_1_, bf16[1024,128]{1,0:T(8,128)(2,1)} %copy-done, bf16[1024,128]{1,0:T(8,128)(2,1)} %get-tuple-element.15.kv_ref.refs_3_, ...), custom_call_target="tpu_custom_call" | custom-call | flops 1342177280 | bytes 20971520 | tf_op jit(solution)/shard_map/pallas_call | solution.py:153
  22.6 3.8 %collective-permute-start.2 = (bf16[512,128]{1,0:T(8,128)(2,1)}, bf16[512,128]{1,0:T(8,128)(2,1)S(1)}, u32[]{:S(2)}, u32[]{:S(2)}) collective-permute-start(bf16[512,128]{1,0:T(8,128)(2,1)} %get-tuple-element.22), channel_id=1, source_target_pairs={{0,12},{4,0},{8,4},{12,8},{1,13},{5,1},{9,5},{13,9},{2,14},{6,2},{... | collective-permute-start | bytes 393224 | tf_op jit(solution)/shard_map/ppermute | solution.py:232
  26.4 0.0 collective-permute-done.1.kv_ref
  26.4 0.0 copy-start.1
  26.4 0.7 %copy-done.1 = bf16[1024,128]{1,0:T(8,128)(2,1)} copy-done((bf16[1024,128]{1,0:T(8,128)(2,1)}, bf16[1024,128]{1,0:T(8,128)(2,1)S(1)}, u32[]{:S(2)}) %copy-start.1) | copy-done | bytes 262168
  27.1 3.6 %shard_map.58 = (f32[512,128]{1,0:T(8,128)}, f32[512,128]{1,0:T(8,128)}) custom-call(f32[2]{0:T(128)} %get-tuple-element.24.scalar_ref, bf16[512,128]{1,0:T(8,128)(2,1)} %bitcast.18, bf16[1024,128]{1,0:T(8,128)(2,1)} %copy-done.1, bf16[512,512]{1,0:T(8,128)(2,1)} %constant.13.clone.upper_ref.refs_1_, f32[512,128]{1,0:T(8,128)} %get-tuple-element.18.refs_0_, ...), custom_call_target="tpu_custom_call" | custom-call | flops 671088640 | bytes 1048576 | tf_op jit(solution)/shard_map/pallas_call | solution.py:187
  30.7 0.0 collective-permute-done.2
  30.7 1.7 %fusion.1 = bf16[1,512,128]{2,1,0:T(8,128)(2,1)} fusion(f32[512,128]{1,0:T(8,128)} %get-tuple-element.20, f32[512,128]{1,0:T(8,128)} %get-tuple-element.21, bf16[512,128]{1,0:T(8,128)(2,1)S(1)} %collective-permute-done.2, pred[]{:T(512)S(6)} %eq.3), kind=kLoop, calls=%fused_computation.2 | loop fusion | flops 327680 | bytes 786433 | tf_op jit(solution)/shard_map/stack | solution.py:244
  (1 shorter events, 0.0 us)
Async XLA Ops:
  1.9 11.6 %collective-permute-start = (bf16[1024,128]{1,0:T(8,128)(2,1)}, bf16[1024,128]{1,0:T(8,128)(2,1)S(1)}, u32[]{:S(2)}, u32[]{:S(2)}) collective-permute-start(bf16[1024,128]{1,0:T(8,128)(2,1)} %get-tuple-element.14), channel_id=1, source_target_pairs={{0,4},{4,8},{8,12},{12,0},{1,5},{5,9},{9,13},{13,1},{2,6},{6,10},{... | collective-permute-start | bytes 786440 | tf_op jit(solution)/shard_map/ppermute | solution.py:219
  13.5 4.0 %copy-start = (bf16[1024,128]{1,0:T(8,128)(2,1)}, bf16[1024,128]{1,0:T(8,128)(2,1)S(1)}, u32[]{:S(2)}) copy-start(bf16[1024,128]{1,0:T(8,128)(2,1)S(1)} %collective-permute-done.refs_2_.refs_5_) | copy-start | bytes 786436
  13.5 12.9 %collective-permute-start.1 = (bf16[1024,128]{1,0:T(8,128)(2,1)S(1)}, bf16[1024,128]{1,0:T(8,128)(2,1)S(1)}, u32[]{:S(2)}, u32[]{:S(2)}) collective-permute-start(bf16[1024,128]{1,0:T(8,128)(2,1)S(1)} %collective-permute-done.refs_2_.refs_5_), channel_id=1, source_target_pairs={{0,4},{4,8},{8,12},{12,0},{1,5},{5,9},{9,13},{13,1},{2,6},{6,10},{... | collective-permute-start | bytes 786440 | tf_op jit(solution)/shard_map/ppermute | solution.py:229
  22.6 8.1 %collective-permute-start.2 = (bf16[512,128]{1,0:T(8,128)(2,1)}, bf16[512,128]{1,0:T(8,128)(2,1)S(1)}, u32[]{:S(2)}, u32[]{:S(2)}) collective-permute-start(bf16[512,128]{1,0:T(8,128)(2,1)} %get-tuple-element.22), channel_id=1, source_target_pairs={{0,12},{4,0},{8,4},{12,8},{1,13},{5,1},{9,5},{13,9},{2,14},{6,2},{... | collective-permute-start | bytes 393224 | tf_op jit(solution)/shard_map/ppermute | solution.py:232
  26.4 0.7 %copy-start.1 = (bf16[1024,128]{1,0:T(8,128)(2,1)}, bf16[1024,128]{1,0:T(8,128)(2,1)S(1)}, u32[]{:S(2)}) copy-start(bf16[1024,128]{1,0:T(8,128)(2,1)S(1)} %collective-permute-done.1.kv_ref) | copy-start | bytes 786436

commit v4 on v3

--- a/solution.py
+++ b/solution.py
@@ -29,48 +29,69 @@
         summed_ref = refs[0].at[rs]
     q_ref = q_all.at[rs]
     keys = kv_ref.shape[0] // 2
-    score = (
-        lax.dot_general(
-            q_ref[...],
-            kv_ref[:keys, :],
-            (((1,), (1,)), ((), ())),
-            preferred_element_type=jnp.float32,
-        )
-        * (scale * LOG2E)
-        + scalar_ref[0] * LOG2E
-    )
-    spent = jnp.maximum(score, 0.0) + jnp.log2(1.0 + jnp.exp2(-jnp.abs(score)))
+
+    def terms():
+        score = (
+            lax.dot_general(
+                q_ref[...],
+                kv_ref[:keys, :],
+                (((1,), (1,)), ((), ())),
+                preferred_element_type=jnp.float32,
+            )
+            * (scale * LOG2E)
+            + scalar_ref[0] * LOG2E
+        )
+        spent = jnp.maximum(score, 0.0) + jnp.log2(1.0 + jnp.exp2(-jnp.abs(score)))
+        if diag:
+            row = r * tile + lax.broadcasted_iota(jnp.int32, (tile, keys), 0)
+            col = lax.broadcasted_iota(jnp.int32, (tile, keys), 1)
+            live = col < row
+            spent = jnp.where(live, spent, 0.0)
+        upper = upper_ref[...]
+        high = spent.astype(jnp.bfloat16)
+        low = (spent - high.astype(jnp.float32)).astype(jnp.bfloat16)
+        later = jnp.dot(high, upper, preferred_element_type=jnp.float32) + jnp.dot(
+            low, upper, preferred_element_type=jnp.float32
+        )
+        weight = jnp.exp2((score - spent) - later)
+        if diag:
+            weight = jnp.where(live, weight, 0.0)
+        part = jnp.dot(
+            weight.astype(jnp.bfloat16), kv_ref[keys:, :], preferred_element_type=jnp.float32
+        )
+        return part, (later[:, 0:1] + spent[:, 0:1]) * LN2
+
     if diag:
-        row = r * tile + lax.broadcasted_iota(jnp.int32, (tile, keys), 0)
-        col = lax.broadcasted_iota(jnp.int32, (tile, keys), 1)
-        live = col < row
-        spent = jnp.where(live, spent, 0.0)
-    upper = upper_ref[...]
-    high = spent.astype(jnp.bfloat16)
-    low = (spent - high.astype(jnp.float32)).astype(jnp.bfloat16)
-    later = jnp.dot(high, upper, preferred_element_type=jnp.float32) + jnp.dot(
-        low, upper, preferred_element_type=jnp.float32
-    )
-    weight = jnp.exp2((score - spent) - later)
-    if diag:
-        weight = jnp.where(live, weight, 0.0)
-    part = jnp.dot(weight.astype(jnp.bfloat16), kv_ref[keys:, :], preferred_element_type=jnp.float32)
-    if mode == "far":
-        summed_ref[...] = part.astype(summed_ref.dtype)
-        return
-    tot = (later[:, 0:1] + spent[:, 0:1]) * LN2
-    if diag:
+        part, tot = terms()
         summed_ref[...] = part
         refs[1].at[rs][...] = tot
         return
     use = scalar_ref[1] > 0.0
-    before = in_spent_ref[...]
-    summed_ref[...] = jnp.where(use, in_summed_ref[...] + jnp.exp(-before) * part, in_summed_ref[...])
-    after = jnp.where(use, before + tot, before)
-    if mode == "final":
-        spent_ref[...] = jnp.broadcast_to(jnp.exp(-after), spent_ref.shape)
-    else:
-        spent_ref[...] = after
+
+    @pl.when(use)
+    def _():
+        part, tot = terms()
+        if mode == "far":
+            summed_ref[...] = part.astype(summed_ref.dtype)
+            return
+        before = in_spent_ref[...]
+        summed_ref[...] = in_summed_ref[...] + jnp.exp(-before) * part
+        after = before + tot
+        if mode == "final":
+            spent_ref[...] = jnp.broadcast_to(jnp.exp(-after), spent_ref.shape)
+        else:
+            spent_ref[...] = after
+
+    @pl.when(jnp.logical_not(use))
+    def _():
+        if mode == "far":
+            summed_ref[...] = jnp.zeros(summed_ref.shape, summed_ref.dtype)
+            return
+        summed_ref[...] = in_summed_ref[...]
+        if mode == "final":
+            spent_ref[...] = jnp.broadcast_to(jnp.exp(-in_spent_ref[...]), spent_ref.shape)
+        else:
+            spent_ref[...] = in_spent_ref[...]
 
 
 def payload_kernel(flag_ref, q_ref, k_ref, v_ref, own_ref, sent_ref):
@@ -217,7 +238,8 @@
         summed, spent = pair_terms(q_own, kv, upper, table[1], (summed, spent))
         return summed.astype(jnp.bfloat16)
     kv = lax.ppermute(sent, "ctx", up)
-    far_task = dict(q=kv, kv=own_kv, scalars=table[0], mode="far", rows=rows)
+    far_gate = jnp.stack([offset, jnp.where(place == 0, 1.0, 0.0)]).astype(jnp.float32)
+    far_task = dict(q=kv, kv=own_kv, scalars=far_gate, mode="far", rows=rows)
     if count > 3:
         far, summed, spent = fused_terms(
             upper,
@@ -226,13 +248,13 @@
     else:
         (far,) = fused_terms(upper, [far_task])
     for step in range(2, count - 1):
-        kv = lax.ppermute(kv, "ctx", up)
+        route = [(i, i + 1) for i in range(step - 1, count - 1)]
+        route += [(i, i) for i in range(step - 1)] + [(count - 1, step - 1)]
+        kv = lax.ppermute(kv, "ctx", route)
         if step < count - 2:
             summed, spent = pair_terms(q_own, kv, upper, table[step], (summed, spent))
     far = lax.ppermute(far, "ctx", down)
-    summed, scale = pair_terms(
-        q_own, kv, upper, table[count - 2], (summed, spent), mode="final"
-    )
+    summed, scale = pair_terms(q_own, kv, upper, table[count - 2], (summed, spent), mode="final")
     out = jnp.where(last, summed + scale * far.astype(jnp.float32), summed)
     return out.astype(jnp.bfloat16)
 

time: 32.6 us -> 30.4 us (0.933)
  Pallas kernels: 13.9 us -> 11.6 us
  other arithmetic: 1.74 us -> 2.41 us
  local copies, waits for them, and re-layouts: 1.99 us -> 1.32 us
    pallas_call x2, Pallas kernels: 6.89 us -> 5.65 us  [pair_terms(): pl.pallas_call(kernel, in_specs=in_specs, out_specs=out_specs, out_shape=...]
    pallas_call x1, Pallas kernels: 5.1 us -> 4.03 us  [fused_terms(): pl.pallas_call(kernel, in_specs=in_specs, out_specs=out_specs, out_shape=...]
    another operation x1 -> x0, local copies, waits for them, and re-layouts: 0.68 us -> none  [fused_terms(): scalars = jnp.stack([t['scalars'] for t in tasks])]
    another operation x0 -> x2, other arithmetic: none -> 0.68 us  [fused_terms(): scalars = jnp.stack([t['scalars'] for t in tasks])]
    ppermute x1, starting transfers between devices: 0.01 us -> 0.67 us  [one_head(): kv = lax.ppermute(kv, 'ctx', route)]
    ppermute x1, starting transfers between devices: 3.81 us -> 3.32 us  [one_head(): far = lax.ppermute(far, 'ctx', down)]
  transfers between devices with their start and end apart: 3 -> 3, of which waited for: 1 -> 1; matrix products, arithmetic and copies ran while one was open for 4% -> 4% of each run, Pallas kernels for 37% -> 32%
where the time goes in v4:
time: 30.4 us; the launch traced here: 30.2 us
  Pallas kernels  11.6 us (38%)
  waiting for transfers between devices  7.19 us (24%)
  starting transfers between devices  7.04 us (23%)
  other arithmetic  2.41 us (8%)
  local copies, waits for them, and re-layouts  1.32 us (4%)
  between operations  0.68 us (2%)
    ppermute x1, waiting for transfers between devices, one_head(): kv = lax.ppermute(sent, 'ctx', up)  7.19 us
    pallas_call x2, Pallas kernels, pair_terms(): pl.pallas_call(kernel, in_specs=in_specs, out_specs=out_specs, out_shape=...  5.65 us
    pallas_call x1, Pallas kernels, fused_terms(): pl.pallas_call(kernel, in_specs=in_specs, out_specs=out_specs, out_shape=...  4.03 us
    ppermute x1, starting transfers between devices, one_head(): far = lax.ppermute(far, 'ctx', down)  3.32 us
    ppermute x1, starting transfers between devices, one_head(): kv = lax.ppermute(sent, 'ctx', up)  3.05 us
    pallas_call x1, Pallas kernels, payloads(): pl.pallas_call(payload_kernel, grid=(1,), in_specs=[pl.BlockSpec(memory_s...  1.88 us
    another operation x1, other arithmetic, on_device(): return jnp.stack(results, axis=0)  1.73 us
    unnamed x4, local copies, waits for them, and re-layouts  0.7 us
  transfers between devices with their start and end apart: 3, of which 1 were waited for; matrix products, arithmetic and copies ran while one was open for 4% of the time, Pallas kernels for 32%

profile of v4, /device:TPU:0, one launch (start us, length us, event | category | flops | bytes accessed | tf_op | source)
XLA Modules:
  0.0 30.2 jit_solution(7751954573387844605)
XLA Ops:
  0.0 1.9 %shard_map.55 = (bf16[1024,128]{1,0:T(8,128)(2,1)}, bf16[1024,128]{1,0:T(8,128)(2,1)}) custom-call(f32[1]{0:T(128)} %bitcast.3.flag_ref, bf16[512,128]{1,0:T(8,128)(2,1)} %bitcast.17, bf16[512,128]{1,0:T(8,128)(2,1)} %bitcast.15, bf16[512,128]{1,0:T(8,128)(2,1)} %bitcast.16), custom_call_target="tpu_custom_call" | custom-call | tf_op jit(solution)/shard_map/pallas_call | solution.py:117
  1.9 3.1 %collective-permute-start = (bf16[1024,128]{1,0:T(8,128)(2,1)}, bf16[1024,128]{1,0:T(8,128)(2,1)S(1)}, u32[]{:S(2)}, u32[]{:S(2)}) collective-permute-start(bf16[1024,128]{1,0:T(8,128)(2,1)} %get-tuple-element.14), channel_id=1, source_target_pairs={{0,4},{4,8},{8,12},{12,0},{1,5},{5,9},{9,13},{13,1},{2,6},{6,10},{... | collective-permute-start | bytes 786440 | tf_op jit(solution)/shard_map/ppermute | solution.py:240
  5.6 0.1 maximum_bitcast_fusion
  5.7 0.6 %fusion.4 = (f32[2]{0:T(128)}, f32[1,2]{1,0:T(1,128)S(1)}, f32[2]{0:T(128)}) fusion(f32[4,1]{1,0:T(4,128)S(1)} %fusion.2, f32[]{:T(128)} %bitcast.14), kind=kLoop, calls=%fused_computation.10 | loop fusion | bytes 44 | tf_op jit(solution)/shard_map/squeeze | solution.py:233
  6.3 7.2 %collective-permute-done.refs_2_.refs_5_ = bf16[1024,128]{1,0:T(8,128)(2,1)S(1)} collective-permute-done((bf16[1024,128]{1,0:T(8,128)(2,1)}, bf16[1024,128]{1,0:T(8,128)(2,1)S(1)}, u32[]{:S(2)}, u32[]{:S(2)}) %collective-permute-start) | collective-permute-done | bytes 262176 | tf_op jit(solution)/shard_map/ppermute | solution.py:240
  13.5 0.0 copy-start
  13.5 0.7 %collective-permute-start.1 = (bf16[1024,128]{1,0:T(8,128)(2,1)S(1)}, bf16[1024,128]{1,0:T(8,128)(2,1)S(1)}, u32[]{:S(2)}, u32[]{:S(2)}) collective-permute-start(bf16[1024,128]{1,0:T(8,128)(2,1)S(1)} %collective-permute-done.refs_2_.refs_5_), channel_id=1, source_target_pairs={{4,8},{8,12},{0,0},{12,4},{5,9},{9,13},{1,1},{13,5},{6,10},{10,14}... | collective-permute-start | bytes 786440 | tf_op jit(solution)/shard_map/ppermute | solution.py:253
  14.2 0.6 %pad_maximum_fusion.refs_0_ = f32[2,2]{1,0:T(2,128)} fusion(f32[1,2]{1,0:T(1,128)S(1)} %get-tuple-element.24, f32[1,2]{1,0:T(1,128)S(1)} %maximum_bitcast_fusion), kind=kLoop, calls=%fused_computation.8 | loop fusion | flops 4 | bytes 32 | tf_op jit(solution)/shard_map/stack | solution.py:150
  14.8 3.3 %shard_map.56 = (f32[512,128]{1,0:T(8,128)}, f32[512,1]{1,0:T(8,128)}) custom-call(f32[2]{0:T(128)} %get-tuple-element.23.scalar_ref, bf16[512,128]{1,0:T(8,128)(2,1)} %bitcast.18, bf16[1024,128]{1,0:T(8,128)(2,1)} %get-tuple-element.15.kv_ref.refs_3_, bf16[512,512]{1,0:T(8,128)(2,1)} %constant.15.clone.upper_ref.refs_1_), custom_call_target="tpu_custom_call" | custom-call | flops 671088640 | bytes 1048576 | tf_op jit(solution)/shard_map/pallas_call | solution.py:208
  18.1 0.0 copy-done
  18.1 4.0 %shard_map.57 = (bf16[512,128]{1,0:T(8,128)(2,1)}, f32[512,128]{1,0:T(8,128)}, f32[512,1]{1,0:T(8,128)}) custom-call(f32[2,2]{1,0:T(2,128)} %pad_maximum_fusion.refs_0_, bf16[512,512]{1,0:T(8,128)(2,1)} %constant.15.clone.upper_ref.refs_1_, bf16[1024,128]{1,0:T(8,128)(2,1)} %copy-done, bf16[1024,128]{1,0:T(8,128)(2,1)} %get-tuple-element.15.kv_ref.refs_3_, ...), custom_call_target="tpu_custom_call" | custom-call | flops 1342177280 | bytes 20971520 | tf_op jit(solution)/shard_map/pallas_call | solution.py:174
  22.1 3.3 %collective-permute-start.2 = (bf16[512,128]{1,0:T(8,128)(2,1)}, bf16[512,128]{1,0:T(8,128)(2,1)S(1)}, u32[]{:S(2)}, u32[]{:S(2)}) collective-permute-start(bf16[512,128]{1,0:T(8,128)(2,1)} %get-tuple-element.22), channel_id=1, source_target_pairs={{0,12},{4,0},{8,4},{12,8},{1,13},{5,1},{9,5},{13,9},{2,14},{6,2},{... | collective-permute-start | bytes 393224 | tf_op jit(solution)/shard_map/ppermute | solution.py:256
  25.4 0.0 collective-permute-done.1.kv_ref
  25.4 0.0 copy-start.1
  25.4 0.7 %copy-done.1 = bf16[1024,128]{1,0:T(8,128)(2,1)} copy-done((bf16[1024,128]{1,0:T(8,128)(2,1)}, bf16[1024,128]{1,0:T(8,128)(2,1)S(1)}, u32[]{:S(2)}) %copy-start.1) | copy-done | bytes 262168
  26.1 2.3 %shard_map.58 = (f32[512,128]{1,0:T(8,128)}, f32[512,128]{1,0:T(8,128)}) custom-call(f32[2]{0:T(128)} %get-tuple-element.25.scalar_ref, bf16[512,128]{1,0:T(8,128)(2,1)} %bitcast.20, bf16[1024,128]{1,0:T(8,128)(2,1)} %copy-done.1, bf16[512,512]{1,0:T(8,128)(2,1)} %constant.15.clone.upper_ref.refs_1_, f32[512,128]{1,0:T(8,128)} %get-tuple-element.18.refs_0_, ...), custom_call_target="tpu_custom_call" | custom-call | flops 671088640 | bytes 1048576 | tf_op jit(solution)/shard_map/pallas_call | solution.py:208
  28.5 0.0 collective-permute-done.2
  28.5 1.7 %fusion.1 = bf16[1,512,128]{2,1,0:T(8,128)(2,1)} fusion(f32[512,128]{1,0:T(8,128)} %get-tuple-element.20, f32[512,128]{1,0:T(8,128)} %get-tuple-element.21, bf16[512,128]{1,0:T(8,128)(2,1)S(1)} %collective-permute-done.2, pred[]{:T(512)S(6)} %eq.6), kind=kLoop, calls=%fused_computation.2 | loop fusion | flops 327680 | bytes 786433 | tf_op jit(solution)/shard_map/stack | solution.py:266
  (1 shorter events, 0.0 us)
Async XLA Ops:
  1.9 11.6 %collective-permute-start = (bf16[1024,128]{1,0:T(8,128)(2,1)}, bf16[1024,128]{1,0:T(8,128)(2,1)S(1)}, u32[]{:S(2)}, u32[]{:S(2)}) collective-permute-start(bf16[1024,128]{1,0:T(8,128)(2,1)} %get-tuple-element.14), channel_id=1, source_target_pairs={{0,4},{4,8},{8,12},{12,0},{1,5},{5,9},{9,13},{13,1},{2,6},{6,10},{... | collective-permute-start | bytes 786440 | tf_op jit(solution)/shard_map/ppermute | solution.py:240
  13.5 4.6 %copy-start = (bf16[1024,128]{1,0:T(8,128)(2,1)}, bf16[1024,128]{1,0:T(8,128)(2,1)S(1)}, u32[]{:S(2)}) copy-start(bf16[1024,128]{1,0:T(8,128)(2,1)S(1)} %collective-permute-done.refs_2_.refs_5_) | copy-start | bytes 786436
  13.5 11.9 %collective-permute-start.1 = (bf16[1024,128]{1,0:T(8,128)(2,1)S(1)}, bf16[1024,128]{1,0:T(8,128)(2,1)S(1)}, u32[]{:S(2)}, u32[]{:S(2)}) collective-permute-start(bf16[1024,128]{1,0:T(8,128)(2,1)S(1)} %collective-permute-done.refs_2_.refs_5_), channel_id=1, source_target_pairs={{4,8},{8,12},{0,0},{12,4},{5,9},{9,13},{1,1},{13,5},{6,10},{10,14}... | collective-permute-start | bytes 786440 | tf_op jit(solution)/shard_map/ppermute | solution.py:253
  22.1 6.4 %collective-permute-start.2 = (bf16[512,128]{1,0:T(8,128)(2,1)}, bf16[512,128]{1,0:T(8,128)(2,1)S(1)}, u32[]{:S(2)}, u32[]{:S(2)}) collective-permute-start(bf16[512,128]{1,0:T(8,128)(2,1)} %get-tuple-element.22), channel_id=1, source_target_pairs={{0,12},{4,0},{8,4},{12,8},{1,13},{5,1},{9,5},{13,9},{2,14},{6,2},{... | collective-permute-start | bytes 393224 | tf_op jit(solution)/shard_map/ppermute | solution.py:256
  25.4 0.7 %copy-start.1 = (bf16[1024,128]{1,0:T(8,128)(2,1)}, bf16[1024,128]{1,0:T(8,128)(2,1)S(1)}, u32[]{:S(2)}) copy-start(bf16[1024,128]{1,0:T(8,128)(2,1)S(1)} %collective-permute-done.1.kv_ref) | copy-start | bytes 786436

commit v5 on v4

--- a/solution.py
+++ b/solution.py
@@ -220,7 +220,6 @@
     count = lax.axis_size("ctx")
     place = lax.axis_index("ctx")
     up = [(i, (i + 1) % count) for i in range(count)]
-    down = [(i, (i - 1) % count) for i in range(count)]
     rows = q_own.shape[0]
     keys = k_own.shape[0]
     upper = jnp.asarray(np.triu(np.ones((keys, keys), np.float32), 1).T, jnp.bfloat16)
@@ -253,7 +252,13 @@
         kv = lax.ppermute(kv, "ctx", route)
         if step < count - 2:
             summed, spent = pair_terms(q_own, kv, upper, table[step], (summed, spent))
-    far = lax.ppermute(far, "ctx", down)
+    swap = [(0, count - 1), (count - 1, 0)]
+    middle = list(range(1, count - 1))
+    swap += [(a, b) for a, b in zip(middle[0::2], middle[1::2])]
+    swap += [(b, a) for a, b in zip(middle[0::2], middle[1::2])]
+    if len(middle) % 2:
+        swap.append((middle[-1], middle[-1]))
+    far = lax.ppermute(far, "ctx", swap)
     summed, scale = pair_terms(q_own, kv, upper, table[count - 2], (summed, spent), mode="final")
     out = jnp.where(last, summed + scale * far.astype(jnp.float32), summed)
     return out.astype(jnp.bfloat16)

time: 30.4 us -> 31 us (1.020)
  waiting for transfers between devices: 7.19 us -> 7.8 us
    ppermute x1, waiting for transfers between devices: 0.01 us -> 0.61 us  [one_head(): far = lax.ppermute(far, 'ctx', swap)]
  transfers between devices with their start and end apart: 3 -> 3, of which waited for: 1 -> 2; matrix products, arithmetic and copies ran while one was open for 4% -> 4% of each run, Pallas kernels for 32% -> 31%
where the time goes in v5:
time: 31 us; the launch traced here: 30.8 us
  Pallas kernels  11.6 us (37%)
  waiting for transfers between devices  7.8 us (25%)
  starting transfers between devices  7.04 us (23%)
  other arithmetic  2.41 us (8%)
  local copies, waits for them, and re-layouts  1.32 us (4%)
  between operations  0.68 us (2%)
    ppermute x1, waiting for transfers between devices, one_head(): kv = lax.ppermute(sent, 'ctx', up)  7.19 us
    pallas_call x2, Pallas kernels, pair_terms(): pl.pallas_call(kernel, in_specs=in_specs, out_specs=out_specs, out_shape=...  5.65 us
    pallas_call x1, Pallas kernels, fused_terms(): pl.pallas_call(kernel, in_specs=in_specs, out_specs=out_specs, out_shape=...  4.03 us
    ppermute x1, starting transfers between devices, one_head(): far = lax.ppermute(far, 'ctx', swap)  3.32 us
    ppermute x1, starting transfers between devices, one_head(): kv = lax.ppermute(sent, 'ctx', up)  3.05 us
    pallas_call x1, Pallas kernels, payloads(): pl.pallas_call(payload_kernel, grid=(1,), in_specs=[pl.BlockSpec(memory_s...  1.88 us
    another operation x1, other arithmetic, on_device(): return jnp.stack(results, axis=0)  1.73 us
    unnamed x4, local copies, waits for them, and re-layouts  0.7 us
  transfers between devices with their start and end apart: 3, of which 2 were waited for; matrix products, arithmetic and copies ran while one was open for 4% of the time, Pallas kernels for 31%

profile of v5, /device:TPU:0, one launch (start us, length us, event | category | flops | bytes accessed | tf_op | source)
XLA Modules:
  0.0 30.8 jit_solution(1473477316565396907)
XLA Ops:
  0.0 1.9 %shard_map.55 = (bf16[1024,128]{1,0:T(8,128)(2,1)}, bf16[1024,128]{1,0:T(8,128)(2,1)}) custom-call(f32[1]{0:T(128)} %bitcast.3.flag_ref, bf16[512,128]{1,0:T(8,128)(2,1)} %bitcast.17, bf16[512,128]{1,0:T(8,128)(2,1)} %bitcast.15, bf16[512,128]{1,0:T(8,128)(2,1)} %bitcast.16), custom_call_target="tpu_custom_call" | custom-call | tf_op jit(solution)/shard_map/pallas_call | solution.py:117
  1.9 3.1 %collective-permute-start = (bf16[1024,128]{1,0:T(8,128)(2,1)}, bf16[1024,128]{1,0:T(8,128)(2,1)S(1)}, u32[]{:S(2)}, u32[]{:S(2)}) collective-permute-start(bf16[1024,128]{1,0:T(8,128)(2,1)} %get-tuple-element.14), channel_id=1, source_target_pairs={{0,4},{4,8},{8,12},{12,0},{1,5},{5,9},{9,13},{13,1},{2,6},{6,10},{... | collective-permute-start | bytes 786440 | tf_op jit(solution)/shard_map/ppermute | solution.py:239
  5.6 0.1 maximum_bitcast_fusion
  5.7 0.6 %fusion.4 = (f32[2]{0:T(128)}, f32[1,2]{1,0:T(1,128)S(1)}, f32[2]{0:T(128)}) fusion(f32[4,1]{1,0:T(4,128)S(1)} %fusion.2, f32[]{:T(128)} %bitcast.14), kind=kLoop, calls=%fused_computation.10 | loop fusion | bytes 44 | tf_op jit(solution)/shard_map/squeeze | solution.py:232
  6.3 7.2 %collective-permute-done.refs_2_.refs_5_ = bf16[1024,128]{1,0:T(8,128)(2,1)S(1)} collective-permute-done((bf16[1024,128]{1,0:T(8,128)(2,1)}, bf16[1024,128]{1,0:T(8,128)(2,1)S(1)}, u32[]{:S(2)}, u32[]{:S(2)}) %collective-permute-start) | collective-permute-done | bytes 262176 | tf_op jit(solution)/shard_map/ppermute | solution.py:239
  13.5 0.0 copy-start
  13.5 0.7 %collective-permute-start.1 = (bf16[1024,128]{1,0:T(8,128)(2,1)S(1)}, bf16[1024,128]{1,0:T(8,128)(2,1)S(1)}, u32[]{:S(2)}, u32[]{:S(2)}) collective-permute-start(bf16[1024,128]{1,0:T(8,128)(2,1)S(1)} %collective-permute-done.refs_2_.refs_5_), channel_id=1, source_target_pairs={{4,8},{8,12},{0,0},{12,4},{5,9},{9,13},{1,1},{13,5},{6,10},{10,14}... | collective-permute-start | bytes 786440 | tf_op jit(solution)/shard_map/ppermute | solution.py:252
  14.2 0.6 %pad_maximum_fusion.refs_0_ = f32[2,2]{1,0:T(2,128)} fusion(f32[1,2]{1,0:T(1,128)S(1)} %get-tuple-element.24, f32[1,2]{1,0:T(1,128)S(1)} %maximum_bitcast_fusion), kind=kLoop, calls=%fused_computation.8 | loop fusion | flops 4 | bytes 32 | tf_op jit(solution)/shard_map/stack | solution.py:150
  14.8 3.3 %shard_map.56 = (f32[512,128]{1,0:T(8,128)}, f32[512,1]{1,0:T(8,128)}) custom-call(f32[2]{0:T(128)} %get-tuple-element.23.scalar_ref, bf16[512,128]{1,0:T(8,128)(2,1)} %bitcast.18, bf16[1024,128]{1,0:T(8,128)(2,1)} %get-tuple-element.15.kv_ref.refs_3_, bf16[512,512]{1,0:T(8,128)(2,1)} %constant.15.clone.upper_ref.refs_1_), custom_call_target="tpu_custom_call" | custom-call | flops 671088640 | bytes 1048576 | tf_op jit(solution)/shard_map/pallas_call | solution.py:208
  18.1 0.0 copy-done
  18.1 4.0 %shard_map.57 = (bf16[512,128]{1,0:T(8,128)(2,1)}, f32[512,128]{1,0:T(8,128)}, f32[512,1]{1,0:T(8,128)}) custom-call(f32[2,2]{1,0:T(2,128)} %pad_maximum_fusion.refs_0_, bf16[512,512]{1,0:T(8,128)(2,1)} %constant.15.clone.upper_ref.refs_1_, bf16[1024,128]{1,0:T(8,128)(2,1)} %copy-done, bf16[1024,128]{1,0:T(8,128)(2,1)} %get-tuple-element.15.kv_ref.refs_3_, ...), custom_call_target="tpu_custom_call" | custom-call | flops 1342177280 | bytes 20971520 | tf_op jit(solution)/shard_map/pallas_call | solution.py:174
  22.1 3.3 %collective-permute-start.2 = (bf16[512,128]{1,0:T(8,128)(2,1)}, bf16[512,128]{1,0:T(8,128)(2,1)S(1)}, u32[]{:S(2)}, u32[]{:S(2)}) collective-permute-start(bf16[512,128]{1,0:T(8,128)(2,1)} %get-tuple-element.22), channel_id=1, source_target_pairs={{0,12},{12,0},{4,8},{8,4},{1,13},{13,1},{5,9},{9,5},{2,14},{14,2},... | collective-permute-start | bytes 393224 | tf_op jit(solution)/shard_map/ppermute | solution.py:261
  25.4 0.0 collective-permute-done.1.kv_ref
  25.4 0.0 copy-start.1
  25.4 0.7 %copy-done.1 = bf16[1024,128]{1,0:T(8,128)(2,1)} copy-done((bf16[1024,128]{1,0:T(8,128)(2,1)}, bf16[1024,128]{1,0:T(8,128)(2,1)S(1)}, u32[]{:S(2)}) %copy-start.1) | copy-done | bytes 262168
  26.1 2.3 %shard_map.58 = (f32[512,128]{1,0:T(8,128)}, f32[512,128]{1,0:T(8,128)}) custom-call(f32[2]{0:T(128)} %get-tuple-element.25.scalar_ref, bf16[512,128]{1,0:T(8,128)(2,1)} %bitcast.20, bf16[1024,128]{1,0:T(8,128)(2,1)} %copy-done.1, bf16[512,512]{1,0:T(8,128)(2,1)} %constant.15.clone.upper_ref.refs_1_, f32[512,128]{1,0:T(8,128)} %get-tuple-element.18.refs_0_, ...), custom_call_target="tpu_custom_call" | custom-call | flops 671088640 | bytes 1048576 | tf_op jit(solution)/shard_map/pallas_call | solution.py:208
  28.5 0.6 %collective-permute-done.2 = bf16[512,128]{1,0:T(8,128)(2,1)S(1)} collective-permute-done((bf16[512,128]{1,0:T(8,128)(2,1)}, bf16[512,128]{1,0:T(8,128)(2,1)S(1)}, u32[]{:S(2)}, u32[]{:S(2)}) %collective-permute-start.2) | collective-permute-done | bytes 131104 | tf_op jit(solution)/shard_map/ppermute | solution.py:261
  29.1 1.7 %fusion.1 = bf16[1,512,128]{2,1,0:T(8,128)(2,1)} fusion(f32[512,128]{1,0:T(8,128)} %get-tuple-element.20, f32[512,128]{1,0:T(8,128)} %get-tuple-element.21, bf16[512,128]{1,0:T(8,128)(2,1)S(1)} %collective-permute-done.2, pred[]{:T(512)S(6)} %eq.6), kind=kLoop, calls=%fused_computation.2 | loop fusion | flops 327680 | bytes 786433 | tf_op jit(solution)/shard_map/stack | solution.py:271
  (1 shorter events, 0.0 us)
Async XLA Ops:
  1.9 11.6 %collective-permute-start = (bf16[1024,128]{1,0:T(8,128)(2,1)}, bf16[1024,128]{1,0:T(8,128)(2,1)S(1)}, u32[]{:S(2)}, u32[]{:S(2)}) collective-permute-start(bf16[1024,128]{1,0:T(8,128)(2,1)} %get-tuple-element.14), channel_id=1, source_target_pairs={{0,4},{4,8},{8,12},{12,0},{1,5},{5,9},{9,13},{13,1},{2,6},{6,10},{... | collective-permute-start | bytes 786440 | tf_op jit(solution)/shard_map/ppermute | solution.py:239
  13.5 4.6 %copy-start = (bf16[1024,128]{1,0:T(8,128)(2,1)}, bf16[1024,128]{1,0:T(8,128)(2,1)S(1)}, u32[]{:S(2)}) copy-start(bf16[1024,128]{1,0:T(8,128)(2,1)S(1)} %collective-permute-done.refs_2_.refs_5_) | copy-start | bytes 786436
  13.5 11.9 %collective-permute-start.1 = (bf16[1024,128]{1,0:T(8,128)(2,1)S(1)}, bf16[1024,128]{1,0:T(8,128)(2,1)S(1)}, u32[]{:S(2)}, u32[]{:S(2)}) collective-permute-start(bf16[1024,128]{1,0:T(8,128)(2,1)S(1)} %collective-permute-done.refs_2_.refs_5_), channel_id=1, source_target_pairs={{4,8},{8,12},{0,0},{12,4},{5,9},{9,13},{1,1},{13,5},{6,10},{10,14}... | collective-permute-start | bytes 786440 | tf_op jit(solution)/shard_map/ppermute | solution.py:252
  22.1 7.0 %collective-permute-start.2 = (bf16[512,128]{1,0:T(8,128)(2,1)}, bf16[512,128]{1,0:T(8,128)(2,1)S(1)}, u32[]{:S(2)}, u32[]{:S(2)}) collective-permute-start(bf16[512,128]{1,0:T(8,128)(2,1)} %get-tuple-element.22), channel_id=1, source_target_pairs={{0,12},{12,0},{4,8},{8,4},{1,13},{13,1},{5,9},{9,5},{2,14},{14,2},... | collective-permute-start | bytes 393224 | tf_op jit(solution)/shard_map/ppermute | solution.py:261
  25.4 0.7 %copy-start.1 = (bf16[1024,128]{1,0:T(8,128)(2,1)}, bf16[1024,128]{1,0:T(8,128)(2,1)S(1)}, u32[]{:S(2)}) copy-start(bf16[1024,128]{1,0:T(8,128)(2,1)S(1)} %collective-permute-done.1.kv_ref) | copy-start | bytes 786436
